TPU v7x, 128 devices: a whole 4x4x4 slice. The times are simulated.
128 devices in a mesh: space: 32 (over x, z, core), feat: 4 (over y).
Axes of the slice: x: 4, y: 4, z: 4, core: 2. Of those that a mesh axis runs over, the one named last changes fastest.
Arguments:
- inputs: bfloat16 [2, 96, 180, 1024], P(None, 'space', None, 'feat'), may hold values from -15 to 15
- cotangent: bfloat16 [2, 96, 180, 1024], P(None, 'space', None, 'feat'), may hold values from -6 to 6
- spec_w1: float32 [2, 8, 128, 128], P(None, 'feat'), may hold values from -0.375 to 0.375
- spec_b1: float32 [2, 1024], P(None, 'feat'), may hold values from -0.3 to 0.3
- spec_w2: float32 [2, 8, 128, 128], P(None, 'feat'), may hold values from -0.375 to 0.375
- spec_b2: float32 [2, 1024], P(None, 'feat'), may hold values from -0.3 to 0.3
- up_weight: bfloat16 [1024, 4096], P(None, 'feat'), may hold values from -0.1875 to 0.1875
- down_weight: bfloat16 [4096, 1024], P('feat'), may hold values from -0.09375 to 0.09375
Outputs:
- output: bfloat16 [2, 96, 180, 1024], P(None, 'space', None, 'feat')
- grad_input: bfloat16 [2, 96, 180, 1024], P(None, 'space', None, 'feat')
All inputs are finite; a program needn't handle non-finite values.
Results may differ from a plain program's by a relative error of at most 0.0102.
Values may be sent and summed in bfloat16 or wider, within the bound.
No kernel may reach another device: no remote copies, remote signals or barrier semaphores. Data moves between devices by JAX's collectives and lax.ppermute only.
A program may use at most 128 MiB of HBM per device.

v0:
```python
import math

import jax
import jax.numpy as jnp
from jax import lax
from jax.sharding import PartitionSpec as P

EPSILON = 1e-05
SHRINK_LEVEL = 0.1
HIGHEST = lax.Precision.HIGHEST


def longitude_tables(width_lon):
    mode_count = width_lon // 2 + 1
    cell_index = jnp.arange(width_lon, dtype=jnp.int32)[:, None]
    wave_number = jnp.arange(mode_count, dtype=jnp.int32)[None, :]
    phase_angle = (
        2.0 * math.pi / width_lon * (cell_index * wave_number % width_lon).astype(jnp.float32)
    )
    scaling = 1.0 / math.sqrt(width_lon)
    cos_fwd = jnp.cos(phase_angle) * scaling
    sin_fwd = -jnp.sin(phase_angle) * scaling
    doubled = jnp.where((wave_number == 0) | (wave_number * 2 == width_lon), 1.0, 2.0).astype(
        jnp.float32
    )
    return (cos_fwd, sin_fwd, cos_fwd * doubled, sin_fwd * doubled)


def padded_tables(width_lon, multiple):
    tables = longitude_tables(width_lon)
    modes = tables[0].shape[1]
    extra = -modes % multiple
    return tuple(jnp.pad(table, ((0, 0), (0, extra))) for table in tables)


def lat_apply(table, field):
    return jnp.einsum("gh,bhkc->bgkc", table, field, precision=HIGHEST)


def complex_latitude(table_cos, table_sin, real_part, imag_part, inverse):
    if inverse:
        return (
            lat_apply(table_cos, real_part) + lat_apply(table_sin, imag_part),
            lat_apply(table_cos, imag_part) - lat_apply(table_sin, real_part),
        )
    return (
        lat_apply(table_cos, real_part) - lat_apply(table_sin, imag_part),
        lat_apply(table_cos, imag_part) + lat_apply(table_sin, real_part),
    )


def lon_forward(field, table):
    return jnp.einsum("brwc,wk->brkc", field, table, precision=HIGHEST)


def lon_back(spec, table):
    return jnp.einsum("brkc,wk->brwc", spec, table, precision=HIGHEST)


def to_blocks(field, block_size):
    return field.reshape(field.shape[:-1] + (field.shape[-1] // block_size, block_size))


def block_mult(field, weights):
    return jnp.einsum("...nc,nce->...ne", field, weights, precision=HIGHEST)


def block_mult_back(field, weights):
    return jnp.einsum("...ne,nce->...nc", field, weights, precision=HIGHEST)


def block_product(real_part, imag_part, weights):
    return (
        block_mult(real_part, weights[0]) - block_mult(imag_part, weights[1]),
        block_mult(real_part, weights[1]) + block_mult(imag_part, weights[0]),
    )


def block_adjoint(real_part, imag_part, weights):
    return (
        block_mult_back(real_part, weights[0]) + block_mult_back(imag_part, weights[1]),
        block_mult_back(imag_part, weights[0]) - block_mult_back(real_part, weights[1]),
    )


def latitude_tables(length):
    index_row = jnp.arange(length, dtype=jnp.int32)
    phase_angle = (
        2.0 * math.pi / length * (index_row[:, None] * index_row[None, :] % length).astype(jnp.float32)
    )
    scaling = 1.0 / math.sqrt(length)
    return (jnp.cos(phase_angle) * scaling, -jnp.sin(phase_angle) * scaling)


def to_columns(real_part, imag_part, link_type):
    stacked = jnp.stack([real_part, imag_part]).astype(link_type)
    moved = lax.all_to_all(stacked, "space", 3, 2, tiled=True).astype(jnp.float32)
    return (moved[0], moved[1])


def to_rows(real_part, imag_part, link_type):
    stacked = jnp.stack([real_part, imag_part]).astype(link_type)
    moved = lax.all_to_all(stacked, "space", 2, 3, tiled=True).astype(jnp.float32)
    return (moved[0], moved[1])


def enter_spectrum(real_part, imag_part, tables_lat, link_type=jnp.float32):
    table_cos, table_sin = tables_lat
    real_part, imag_part = to_columns(real_part, imag_part, link_type)
    return complex_latitude(table_cos, table_sin, real_part, imag_part, False)


def leave_spectrum(real_part, imag_part, tables_lat, link_type=jnp.float32):
    table_cos, table_sin = tables_lat
    real_part, imag_part = complex_latitude(table_cos, table_sin, real_part, imag_part, True)
    return to_rows(real_part, imag_part, link_type)


def complex_operator(real_block, imag_block):
    return jnp.stack(
        [jnp.stack([real_block, -imag_block]), jnp.stack([imag_block, real_block])]
    )


def lat_stacked(operator, field, precision=lax.Precision.HIGH):
    return jnp.einsum("pqkh,qbhlc->pbklc", operator, field, precision=precision)


def lon_stacked_forward(field, tables, precision=lax.Precision.HIGH):
    return jnp.einsum("brwc,pwk->pbrkc", field, tables, precision=precision)


def lon_stacked_back(spec, tables, precision=lax.Precision.HIGH):
    return jnp.einsum("pbrkc,pwk->brwc", spec, tables, precision=precision)


def block_operator(weights):
    return jnp.moveaxis(complex_operator(weights[0], weights[1]), 2, 0)


def block_stacked(field, operator):
    return jnp.einsum("qbklnc,npqce->pbklne", field, operator, precision=lax.Precision.HIGH)


def block_stacked_adjoint(field, operator):
    return jnp.einsum("pbklne,npqce->qbklnc", field, operator, precision=lax.Precision.DEFAULT)


def stacked_columns(field, link_type):
    return lax.all_to_all(field.astype(link_type), "space", 3, 2, tiled=True).astype(jnp.float32)


def stacked_rows(field, link_type):
    return lax.all_to_all(field.astype(link_type), "space", 2, 3, tiled=True).astype(jnp.float32)


def token_sums(first_term, second_term):
    pair = jnp.stack([first_term, second_term])
    count = lax.axis_size("feat")
    position = lax.axis_index("feat")
    shifted = jnp.stack(
        [pair]
        + [
            lax.ppermute(pair, "feat", [(i, (i + count - shift) % count) for i in range(count)])
            for shift in range(1, count)
        ]
    )
    ordered = shifted[(jnp.arange(count) + count - position) % count]
    total = ordered[0]
    for source in range(1, count):
        total = total + ordered[source]
    return (total[0], total[1])


def ring_send(block):
    count = lax.axis_size("feat")
    return [block] + [
        lax.ppermute(block, "feat", [(i, (i + shift) % count) for i in range(count)])
        for shift in range(1, count)
    ]


def ring_assemble(parts):
    count = len(parts)
    position = lax.axis_index("feat")
    block = parts[0]
    width = block.shape[-1]
    whole = jnp.zeros(block.shape[:-1] + (width * count,), block.dtype)
    for shift, moved in enumerate(parts):
        source = (position + count - shift) % count
        whole = lax.dynamic_update_slice_in_dim(whole, moved, source * width, axis=block.ndim - 1)
    return whole


def channel_share(term):
    return lax.psum_scatter(
        term.astype(jnp.bfloat16), "feat", scatter_dimension=3, tiled=True
    ).astype(jnp.float32)


def gelu_value(field):
    return 0.5 * field * (1.0 + lax.erf(field * (1.0 / math.sqrt(2.0))))


def gelu_slope(field):
    return 0.5 * (1.0 + lax.erf(field * (1.0 / math.sqrt(2.0)))) + field * jnp.exp(
        -0.5 * field * field
    ) * (1.0 / math.sqrt(2.0 * math.pi))


def per_device(inputs, cotangent, spec_w1, spec_b1, spec_w2, spec_b2, up_weight, down_weight):
    full_width = up_weight.shape[0]
    block_size = spec_w1.shape[2]
    tables_lon = padded_tables(inputs.shape[2], lax.axis_size("space"))
    tables_lat = latitude_tables(inputs.shape[1] * lax.axis_size("space"))
    cos_fwd, sin_fwd, cos_inv, sin_inv = tables_lon
    table_cos, table_sin = tables_lat
    operators = (
        jnp.stack([cos_fwd, sin_fwd]),
        jnp.stack([cos_inv, sin_inv]),
        complex_operator(table_cos, table_sin),
        complex_operator(table_cos, -table_sin),
        block_operator(spec_w1),
        block_operator(spec_w2),
    )
    operators = lax.optimization_barrier(operators)
    lon_fwd_tables, lon_inv_tables, lat_forward_op, lat_inverse_op, first_op, second_op = operators
    values = inputs.astype(jnp.float32)
    cotangent_parts = ring_send(cotangent)
    first_sum, second_sum = token_sums(jnp.sum(values, axis=-1), jnp.sum(values * values, axis=-1))
    mean_one = first_sum[..., None] / full_width
    rstd_one = lax.rsqrt(second_sum[..., None] / full_width - mean_one * mean_one + EPSILON)
    normed = (values - mean_one) * rstd_one
    spec = lat_stacked(
        lat_forward_op, stacked_columns(lon_stacked_forward(normed, lon_fwd_tables), jnp.float32)
    )
    spec_blocks = to_blocks(spec, block_size)
    bias_one = to_blocks(spec_b1, block_size)[:, None, None, None]
    bias_two = to_blocks(spec_b2, block_size)[:, None, None, None]
    first = jax.nn.relu(block_stacked(spec_blocks, first_op) + bias_one)
    second = block_stacked(first, second_op) + bias_two
    shrunk = (second - jnp.clip(second, -SHRINK_LEVEL, SHRINK_LEVEL)).reshape(spec.shape)
    shrunk, cotangent_parts = lax.optimization_barrier((shrunk, cotangent_parts))
    whole_cotangent = ring_assemble(cotangent_parts)
    filtered = lon_stacked_back(
        stacked_rows(lat_stacked(lat_inverse_op, shrunk), jnp.bfloat16), lon_inv_tables
    )
    residual = (filtered + normed + values).astype(jnp.bfloat16)
    residual_vals = residual.astype(jnp.float32)
    whole_residual = lax.all_gather(residual, "feat", axis=3, tiled=True)
    grad_act = jnp.einsum(
        "brwd,hd->brwh", whole_cotangent, down_weight, preferred_element_type=jnp.float32
    )
    whole_residual, grad_act = lax.optimization_barrier((whole_residual, grad_act))
    whole_vals = whole_residual.astype(jnp.float32)
    mean_two = jnp.sum(whole_vals, axis=-1, keepdims=True) / full_width
    square_two = jnp.sum(whole_vals * whole_vals, axis=-1, keepdims=True) / full_width
    rstd_two = lax.rsqrt(square_two - mean_two * mean_two + EPSILON)
    vhat = (whole_vals - mean_two) * rstd_two
    hidden = jnp.einsum(
        "brwd,dh->brwh", vhat.astype(jnp.bfloat16), up_weight, preferred_element_type=jnp.float32
    )
    activated = gelu_value(hidden).astype(jnp.bfloat16)
    mixed_term = jnp.einsum(
        "brwh,hd->brwd", activated, down_weight, preferred_element_type=jnp.float32
    )
    output = (residual_vals + channel_share(mixed_term)).astype(jnp.bfloat16)
    grad_hidden = (grad_act * gelu_slope(hidden)).astype(jnp.bfloat16)
    grad_term = jnp.einsum(
        "brwh,dh->brwd", grad_hidden, up_weight, preferred_element_type=jnp.float32
    )
    total_one, total_two = token_sums(
        jnp.sum(grad_term, axis=-1), jnp.sum(grad_term * vhat, axis=-1)
    )
    grad_vhat = channel_share(grad_term)
    own_hat = (residual_vals - mean_two) * rstd_two
    grad_residual = cotangent.astype(jnp.float32) + rstd_two * (
        grad_vhat
        - total_one[..., None] / full_width
        - own_hat * (total_two[..., None] / full_width)
    )
    grad_spec = lat_stacked(
        lat_forward_op,
        stacked_columns(
            lon_stacked_forward(grad_residual, lon_inv_tables, lax.Precision.DEFAULT), jnp.bfloat16
        ),
        lax.Precision.DEFAULT,
    )
    grad_second = jnp.where(
        jnp.abs(second) > SHRINK_LEVEL, to_blocks(grad_spec, block_size), 0.0
    )
    grad_first = jnp.where(first > 0.0, block_stacked_adjoint(grad_second, second_op), 0.0)
    grad_spectrum = block_stacked_adjoint(grad_first, first_op).reshape(spec.shape)
    grad_normed = grad_residual + lon_stacked_back(
        stacked_rows(
            lat_stacked(lat_inverse_op, grad_spectrum, lax.Precision.DEFAULT), jnp.bfloat16
        ),
        lon_fwd_tables,
        lax.Precision.DEFAULT,
    )
    norm_one, norm_two = token_sums(
        jnp.sum(grad_normed, axis=-1), jnp.sum(grad_normed * normed, axis=-1)
    )
    grad_input = grad_residual + rstd_one * (
        grad_normed - norm_one[..., None] / full_width - normed * (norm_two[..., None] / full_width)
    )
    return (output, grad_input.astype(jnp.bfloat16))


def solution(mesh):
    return jax.shard_map(
        per_device,
        mesh=mesh,
        in_specs=(
            P(None, "space", None, "feat"),
            P(None, "space", None, "feat"),
            P(None, "feat", None, None),
            P(None, "feat"),
            P(None, "feat", None, None),
            P(None, "feat"),
            P(None, "feat"),
            P("feat", None),
        ),
        out_specs=(P(None, "space", None, "feat"), P(None, "space", None, "feat")),
        check_vma=False,
    )
```

profile of v0, /device:TPU:0, one launch (start us, length us, event | category | flops | bytes accessed | tf_op | source)
XLA Modules:
  0.0 234.4 jit_solution(12119883770592294204)
XLA Ops:
  7.2 1.7 convert_reduce_fusion.1
  9.5 3.3 %collective-permute-start.1 = (f32[2,2,3,180]{3,2,1,0:T(4,128)}, f32[2,2,3,180]{3,2,1,0:T(4,128)}, u32[]{:S(2)}, u32[]{:S(2)}) collective-permute-start(f32[2,2,3,180]{3,2,1,0:T(4,128)} %get-tuple-element.72), channel_id=1, source_target_pairs={{0,2},{1,3},{2,0},{3,1},{4,6},{5,7},{6,4},{7,5},{8,10},{9,11},{10,... | collective-permute-start | bytes 25928 | tf_op jit(solution)/shard_map/ppermute | solution.py:164
  12.8 1.1 collective-permute-start
  13.8 1.0 collective-permute-start.2
  21.0 1.1 maximum_bitcast_fusion.1
  23.5 1.9 convolution_bitcast_fusion.7
  25.4 2.0 copy.105
  27.4 8.2 %all-to-all-start = ((f32[2,2,3,96,256]{4,1,2,0,3:T(2,128)}), f32[2,2,3,96,256]{4,1,2,0,3:T(2,128)S(1)}, u32[]{:S(2)}, u32[]{:S(2)}) async-start(f32[2,2,3,96,256]{4,1,2,0,3:T(2,128)} %copy.105), calls=%async_computation | async-start | bytes 2359296 | tf_op jit(solution)/shard_map/all_to_all | solution.py:150
  35.7 2.3 collective-permute-start.5
  38.9 15.0 %all-to-all-done = f32[2,2,3,96,256]{4,1,2,0,3:T(2,128)S(1)} async-done(((f32[2,2,3,96,256]{4,1,2,0,3:T(2,128)}), f32[2,2,3,96,256]{4,1,2,0,3:T(2,128)S(1)}, u32[]{:S(2)}, u32[]{:S(2)}) %all-to-all-start) | async-done | bytes 1179680 | tf_op jit(solution)/shard_map/all_to_all | solution.py:150
  54.0 1.1 copy-done.5
  55.0 1.7 copy.107
  56.7 1.8 convolution_bitcast_fusion.6
  58.5 2.8 %reshape.280 = f32[2,2,96,3,2,128]{5,4,2,0,3,1:T(2,128)} reshape(f32[2,2,96,3,256]{4,2,0,3,1:T(8,128)} %convolution_bitcast_fusion.6) | data formatting | bytes 2359296 | tf_op jit(solution)/shard_map/reshape | solution.py:61
  61.3 2.1 fusion.30
  64.2 0.9 copy-done.1
  65.2 0.8 collective-permute-done.3
  67.3 19.0 %all_to_all.72 = bf16[2,2,96,3,256]{4,0,3,1,2:T(2,128)(2,1)S(1)} all-to-all(bf16[2,2,96,3,256]{4,0,3,1,2:T(2,128)(2,1)S(1)} %copy.117), channel_id=1, replica_groups=mesh['space'=32,'feat'=4] {'space'}, dimensions={2} | all-to-all | bytes 1179648 | tf_op jit(solution)/shard_map/all_to_all | solution.py:154
  86.8 1.5 fusion.36
  89.8 1.2 copy_dynamic-update-slice_fusion.2
  91.0 1.3 copy_dynamic-update-slice_fusion.1
  92.3 1.2 copy_dynamic-update-slice_fusion
  93.5 4.7 %fusion.23 = f32[2,3,180,1024]{3,2,1,0:T(8,128)} fusion(bf16[2,3,180,1024]{3,2,1,0:T(8,128)(2,1)S(1)} %copy_dynamic-update-slice_fusion, bf16[1024,1024]{1,0:T(8,128)(2,1)S(1)} %copy-done.30), kind=kOutput, calls=%fused_computation.30 | convolution fusion | flops 2264924160 | bytes 8732672 | tf_op jit(solution)/shard_map/brwd,hd->brwh/dot_general | solution.py:251
  98.2 22.0 %all-gather.2.cloned.1.call-done = bf16[2,3,180,1024]{3,2,1,0:T(8,128)(2,1)} async-done(((bf16[2,3,180,256]{3,2,1,0:T(8,128)(2,1)}), bf16[2,3,180,1024]{3,2,1,0:T(8,128)(2,1)}) %all-gather.2.cloned.1.call-update) | async-done | bytes 2211856 | tf_op jit(solution)/shard_map/all_gather | solution.py:250
  120.2 2.5 %convert_reduce_fusion = (f32[2,3,180]{2,1,0:T(4,128)S(1)}, f32[2,3,180]{2,1,0:T(4,128)S(1)}) fusion(bf16[2,3,180,1024]{3,2,1,0:T(8,128)(2,1)} %all-gather.2.cloned.1.call-done), kind=kLoop, calls=%fused_computation.6 | loop fusion | flops 4421520 | bytes 2220480 | tf_op jit(solution)/shard_map/reduce_sum | solution.py:256
  122.8 2.8 %fusion.14 = f32[2,3,180,1024]{3,2,1,0:T(8,128)S(1)} fusion(bf16[2,3,180,1024]{3,2,1,0:T(8,128)(2,1)S(1)} %copy-done.10, f32[2,3,180]{2,1,0:T(4,128)S(1)} %get-tuple-element.74, f32[2,3,180]{2,1,0:T(4,128)S(1)} %get-tuple-element.73, bf16[1024,1024]{1,0:T(8,128)(2,1)S(1)} %copy-done), kind=kOutput, calls=%fused_computation.22 | convolution fusion | flops 2269347840 | bytes 8741312 | tf_op jit(solution)/shard_map/brwd,dh->brwh/dot_general | solution.py:260
  125.8 5.4 %fusion.127 = (f32[2,3,180]{2,1,0:T(4,128)S(1)}, f32[2,3,180]{2,1,0:T(4,128)S(1)}, bf16[2,3,180,1024]{3,2,1,0:T(8,128)(2,1)}) fusion(f32[2,3,180]{2,1,0:T(4,128)S(1)} %get-tuple-element.74, f32[2,3,180]{2,1,0:T(4,128)S(1)} %get-tuple-element.73, bf16[2,3,180,1024]{3,2,1,0:T(8,128)(2,1)S(1)} %copy-done.10, bf16[1024,1024]{1,0:T(8,128)(2,1)S(1)} %copy-done, ...), kind=kOutput, calls=%fused_computation.214 | convolution fusion | flops 2283722752 | bytes 15385472 | tf_op jit(solution)/shard_map/brwh,dh->brwd/dot_general | solution.py:269
  131.2 6.9 %fusion.27 = bf16[2,3,180,1024]{3,2,1,0:T(8,128)(2,1)} fusion(bf16[1024,1024]{1,0:T(8,128)(2,1)} %param.15, f32[2,3,180,1024]{3,2,1,0:T(8,128)} %copy-done.31), kind=kOutput, calls=%fused_computation.38 | convolution fusion | flops 2271559680 | bytes 8732672 | tf_op jit(solution)/shard_map/brwh,hd->brwd/dot_general | solution.py:264
  138.2 2.8 %collective-permute-start.7 = (f32[2,2,3,180]{3,2,1,0:T(4,128)S(1)}, f32[2,2,3,180]{3,2,1,0:T(4,128)S(1)}, u32[]{:S(2)}, u32[]{:S(2)}) collective-permute-start(f32[2,2,3,180]{3,2,1,0:T(4,128)S(1)} %get-tuple-element.70), channel_id=1, source_target_pairs={{0,2},{1,3},{2,0},{3,1},{4,6},{5,7},{6,4},{7,5},{8,10},{9,11},{10,... | collective-permute-start | bytes 25928 | tf_op jit(solution)/shard_map/ppermute | solution.py:164
  141.7 1.3 collective-permute-start.8
  143.5 1.4 collective-permute-done.6
  144.9 2.0 collective-permute-done.8
  147.6 1.5 gather_fusion.1
  149.2 14.4 %reduce-scatter.5.cloned.1.call-done = bf16[2,3,180,256]{3,2,1,0:T(8,128)(2,1)} async-done(((bf16[2,3,180,1024]{3,2,1,0:T(8,128)(2,1)}), bf16[2,3,180,256]{3,2,1,0:T(8,128)(2,1)}) %reduce-scatter.5.cloned.1.call-update) | async-done | bytes 552976 | tf_op jit(solution)/shard_map/reduce_scatter | solution.py:196
  163.6 2.4 %fusion.39 = bf16[2,2,3,96,256]{4,3,2,1,0:T(8,128)(2,1)S(1)} fusion(bf16[2,3,180,256]{3,2,1,0:T(8,128)(2,1)} %fusion.36, bf16[2,3,180,256]{3,2,1,0:T(8,128)(2,1)} %reduce-scatter.5.cloned.1.call-done, bf16[2,3,180,256]{3,0,2,1:T(2,128)(2,1)} %param.9, f32[2,3,180]{2,1,0:T(4,128)S(1)} %get-tuple-element.68, f32[2,3,180]{2,1,0:T(4,128)} %copy-done.23, ...), kind=kOutput, calls=%fused_computation.63 | convolution fusion | flops 108933120 | bytes 2404224 | tf_op jit(solution)/shard_map/brwc,pwk->pbrkc/dot_general | solution.py:130
  166.6 18.8 %all_to_all.73 = bf16[2,2,3,96,256]{4,1,2,0,3:T(2,128)(2,1)S(1)} all-to-all(bf16[2,2,3,96,256]{4,1,2,0,3:T(2,128)(2,1)S(1)} %copy.126), channel_id=1, replica_groups=mesh['space'=32,'feat'=4] {'space'}, dimensions={3} | all-to-all | bytes 1179648 | tf_op jit(solution)/shard_map/all_to_all | solution.py:150
  185.8 1.2 convolution_bitcast_fusion.8
  187.0 2.5 %reshape.338 = bf16[2,2,96,3,2,128]{5,4,2,0,3,1:T(2,128)(2,1)} reshape(bf16[2,2,96,3,256]{4,2,0,3,1:T(8,128)(2,1)} %convolution_bitcast_fusion.8) | data formatting | bytes 1179648 | tf_op jit(solution)/shard_map/reshape | solution.py:61
  189.6 2.1 fusion.38
  194.1 15.9 %all_to_all.74 = bf16[2,2,96,3,256]{4,0,3,1,2:T(2,128)(2,1)S(1)} all-to-all(bf16[2,2,96,3,256]{4,0,3,1,2:T(2,128)(2,1)S(1)} %copy.138), channel_id=1, replica_groups=mesh['space'=32,'feat'=4] {'space'}, dimensions={2} | all-to-all | bytes 1179648 | tf_op jit(solution)/shard_map/all_to_all | solution.py:154
  210.5 2.8 %fusion.128 = (f32[2,3,180]{2,1,0:T(4,128)S(1)}, f32[2,3,180]{2,1,0:T(4,128)S(1)}, f32[2,3,180,256]{3,2,1,0:T(8,128)}) fusion(f32[2,3,180]{2,1,0:T(4,128)S(1)} %fusion.114, f32[2,3,180]{2,1,0:T(4,128)S(1)} %fusion.115, bf16[2,3,180,256]{3,0,2,1:T(2,128)(2,1)S(1)} %copy-done.4, bf16[2,2,3,96,256]{4,1,3,2,0:T(2,128)(2,1)S(1)} %bitcast.320, ...), kind=kOutput, calls=%fused_computation.215 | convolution fusion | flops 110866320 | bytes 4080384 | tf_op jit(solution)/shard_map/pbrkc,pwk->brwc/dot_general | solution.py:134
  213.3 1.3 collective-permute-start.10
  214.6 1.6 collective-permute-start.9
  216.6 2.0 collective-permute-done.10
  218.6 2.6 %collective-permute-done.11 = f32[2,2,3,180]{3,2,1,0:T(4,128)S(1)} collective-permute-done((f32[2,2,3,180]{3,2,1,0:T(4,128)S(1)}, f32[2,2,3,180]{3,2,1,0:T(4,128)S(1)}, u32[]{:S(2)}, u32[]{:S(2)}) %collective-permute-start.11) | collective-permute-done | bytes 8672 | tf_op jit(solution)/shard_map/ppermute | solution.py:164
  222.0 3.4 %fusion.67 = (bf16[2,3,180,256]{3,2,1,0:T(8,128)(2,1)S(1)}, bf16[2,3,180,256]{3,2,1,0:T(8,128)(2,1)S(1)}) fusion(f32[2,3,180,256]{3,2,1,0:T(8,128)} %get-tuple-element.78, f32[2,3,180]{2,1,0:T(4,128)S(1)} %get-tuple-element.64, f32[2,3,180]{2,1,0:T(4,128)S(1)} %get-tuple-element.63, f32[2,3,180]{2,1,0:T(4,128)S(1)} %fusion.114, ...), kind=kLoop, calls=%fused_computation.94 | loop fusion | flops 6082560 | bytes 5011200 | tf_op jit(solution)/shard_map/convert_element_type | solution.py:307
  225.4 1.2 copy.143
  226.6 1.2 copy.142
  (135 shorter events, 20.0 us)
Async XLA Ops:
  7.2 115.7 %copy-start = (bf16[1024,1024]{1,0:T(8,128)(2,1)S(1)}, bf16[1024,1024]{1,0:T(8,128)(2,1)}, u32[]{:S(2)}) copy-start(bf16[1024,1024]{1,0:T(8,128)(2,1)} %param.14) | copy-start | bytes 6291460
  7.2 11.4 %copy-start.17 = (f32[2,2,128,128]{3,2,1,0:T(8,128)S(1)}, f32[2,2,128,128]{3,2,1,0:T(8,128)}, u32[]{:S(2)}) copy-start(f32[2,2,128,128]{3,2,1,0:T(8,128)} %param.10) | copy-start | bytes 786436
  7.2 11.4 %copy-start.18 = (f32[2,2,128,128]{3,2,1,0:T(8,128)S(1)}, f32[2,2,128,128]{3,2,1,0:T(8,128)}, u32[]{:S(2)}) copy-start(f32[2,2,128,128]{3,2,1,0:T(8,128)} %param.12) | copy-start | bytes 786436
  9.5 12.5 %collective-permute-start.1 = (f32[2,2,3,180]{3,2,1,0:T(4,128)}, f32[2,2,3,180]{3,2,1,0:T(4,128)}, u32[]{:S(2)}, u32[]{:S(2)}) collective-permute-start(f32[2,2,3,180]{3,2,1,0:T(4,128)} %get-tuple-element.72), channel_id=1, source_target_pairs={{0,2},{1,3},{2,0},{3,1},{4,6},{5,7},{6,4},{7,5},{8,10},{9,11},{10,... | collective-permute-start | bytes 25928 | tf_op jit(solution)/shard_map/ppermute | solution.py:164
  12.8 9.3 %collective-permute-start = (f32[2,2,3,180]{3,2,1,0:T(4,128)}, f32[2,2,3,180]{3,2,1,0:T(4,128)}, u32[]{:S(2)}, u32[]{:S(2)}) collective-permute-start(f32[2,2,3,180]{3,2,1,0:T(4,128)} %get-tuple-element.72), channel_id=1, source_target_pairs={{0,3},{1,0},{2,1},{3,2},{4,7},{5,4},{6,5},{7,6},{8,11},{9,8},{10,9... | collective-permute-start | bytes 25928 | tf_op jit(solution)/shard_map/ppermute | solution.py:164
  13.8 8.2 %collective-permute-start.2 = (f32[2,2,3,180]{3,2,1,0:T(4,128)}, f32[2,2,3,180]{3,2,1,0:T(4,128)}, u32[]{:S(2)}, u32[]{:S(2)}) collective-permute-start(f32[2,2,3,180]{3,2,1,0:T(4,128)} %get-tuple-element.72), channel_id=1, source_target_pairs={{0,1},{1,2},{2,3},{3,0},{4,5},{5,6},{6,7},{7,4},{8,9},{9,10},{10,1... | collective-permute-start | bytes 25928 | tf_op jit(solution)/shard_map/ppermute | solution.py:164
  18.6 1.5 copy-start.19
  18.6 1.5 copy-start.20
  18.6 1.5 copy-start.21
  21.0 2.5 %copy-start.2 = (bf16[2,3,180,256]{3,0,2,1:T(2,128)(2,1)S(1)}, bf16[2,3,180,256]{3,0,2,1:T(2,128)(2,1)}, u32[]{:S(2)}) copy-start(bf16[2,3,180,256]{3,0,2,1:T(2,128)(2,1)} %param.8) | copy-start | bytes 1658884
  22.0 5.4 %copy-start.27 = (s32[1024]{0:T(1024)}, s32[1024]{0:T(1024)S(1)}, u32[]{:S(2)}) copy-start(s32[1024]{0:T(1024)S(1)} %pad_clamp_fusion) | copy-start | bytes 12292
  27.4 26.5 %all-to-all-start = ((f32[2,2,3,96,256]{4,1,2,0,3:T(2,128)}), f32[2,2,3,96,256]{4,1,2,0,3:T(2,128)S(1)}, u32[]{:S(2)}, u32[]{:S(2)}) async-start(f32[2,2,3,96,256]{4,1,2,0,3:T(2,128)} %copy.105), calls=%async_computation | async-start | bytes 2359296 | tf_op jit(solution)/shard_map/all_to_all | solution.py:150
  35.6 84.6 %all-gather.2.cloned.1.call-start = ((), (), s32[]{:S(2)}) async-start(), calls=%async_computation.6 | async-start | bytes 2826240 | tf_op jit(solution)/shard_map/all_gather | solution.py:250
  35.7 29.5 %collective-permute-start.5 = (bf16[2,3,180,256]{3,0,2,1:T(2,128)(2,1)}, bf16[2,3,180,256]{3,0,2,1:T(2,128)(2,1)}, u32[]{:S(2)}, u32[]{:S(2)}) collective-permute-start(bf16[2,3,180,256]{3,0,2,1:T(2,128)(2,1)} %param.9), channel_id=1, source_target_pairs={{0,3},{1,0},{2,1},{3,2},{4,7},{5,4},{6,5},{7,6},{8,11},{9,8},{10,9... | collective-permute-start | bytes 1658888 | tf_op jit(solution)/shard_map/ppermute | solution.py:178
  38.0 27.2 %collective-permute-start.4 = (bf16[2,3,180,256]{3,0,2,1:T(2,128)(2,1)}, bf16[2,3,180,256]{3,0,2,1:T(2,128)(2,1)}, u32[]{:S(2)}, u32[]{:S(2)}) collective-permute-start(bf16[2,3,180,256]{3,0,2,1:T(2,128)(2,1)} %param.9), channel_id=1, source_target_pairs={{0,2},{1,3},{2,0},{3,1},{4,6},{5,7},{6,4},{7,5},{8,10},{9,11},{10,... | collective-permute-start | bytes 1658888 | tf_op jit(solution)/shard_map/ppermute | solution.py:178
  38.5 27.5 %collective-permute-start.3 = (bf16[2,3,180,256]{3,0,2,1:T(2,128)(2,1)}, bf16[2,3,180,256]{3,0,2,1:T(2,128)(2,1)}, u32[]{:S(2)}, u32[]{:S(2)}) collective-permute-start(bf16[2,3,180,256]{3,0,2,1:T(2,128)(2,1)} %param.9), channel_id=1, source_target_pairs={{0,1},{1,2},{2,3},{3,0},{4,5},{5,6},{6,7},{7,4},{8,9},{9,10},{10,1... | collective-permute-start | bytes 1658888 | tf_op jit(solution)/shard_map/ppermute | solution.py:178
  54.0 1.1 copy-start.5
  58.5 2.8 %copy-start.28 = (f32[2,256]{1,0:T(2,128)S(1)}, f32[2,256]{1,0:T(2,128)}, u32[]{:S(2)}) copy-start(f32[2,256]{1,0:T(2,128)} %param.11) | copy-start | bytes 6148
  61.3 2.1 copy-start.7
  61.3 2.1 copy-start.29
  64.1 1.9 copy-start.13
  67.3 19.5 %copy-start.3 = (bf16[2,3,180,256]{3,0,2,1:T(2,128)(2,1)S(1)}, bf16[2,3,180,256]{3,0,2,1:T(2,128)(2,1)}, u32[]{:S(2)}) copy-start(bf16[2,3,180,256]{3,0,2,1:T(2,128)(2,1)} %param.8) | copy-start | bytes 1658884
  67.3 19.5 %copy-start.22 = (f32[2,180,96]{2,1,0:T(8,128)S(1)}, f32[2,180,96]{2,1,0:T(8,128)}, u32[]{:S(2)}) copy-start(f32[2,180,96]{2,1,0:T(8,128)} %pad_maximum_fusion.3) | copy-start | bytes 414724
  88.4 75.2 %reduce-scatter.5.cloned.1.call-start = ((), (), s32[]{:S(2)}) async-start(), calls=%async_computation.8 | async-start | bytes 2826240 | tf_op jit(solution)/shard_map/reduce_scatter | solution.py:196
  88.7 1.1 copy-start.11
  91.0 2.5 %copy-start.30 = (bf16[1024,1024]{1,0:T(8,128)(2,1)S(1)}, bf16[1024,1024]{1,0:T(8,128)(2,1)}, u32[]{:S(2)}) copy-start(bf16[1024,1024]{1,0:T(8,128)(2,1)} %param.15) | copy-start | bytes 6291460
  120.2 2.6 %copy-start.10 = (bf16[2,3,180,1024]{3,2,1,0:T(8,128)(2,1)S(1)}, bf16[2,3,180,1024]{3,2,1,0:T(8,128)(2,1)}, u32[]{:S(2)}) copy-start(bf16[2,3,180,1024]{3,2,1,0:T(8,128)(2,1)} %all-gather.2.cloned.1.call-done) | copy-start | bytes 6635524
  120.2 5.5 %slice-start = ((s8[4521984]{0:T(1024)(128)(4,1)}), s8[4194304]{0:T(1024)(128)(4,1)S(1)}, s32[]{:S(2)}) async-start(s8[4521984]{0:T(1024)(128)(4,1)} %bitcast.336), calls=%async_computation.9 | async-start | bytes 8388608
  122.8 2.9 %copy-start.23 = (f32[2,3,180]{2,1,0:T(4,128)}, f32[2,3,180]{2,1,0:T(4,128)S(1)}, u32[]{:S(2)}) copy-start(f32[2,3,180]{2,1,0:T(4,128)S(1)} %get-tuple-element.73) | copy-start | bytes 12964
  122.8 2.9 %copy-start.25 = (f32[2,3,180]{2,1,0:T(4,128)}, f32[2,3,180]{2,1,0:T(4,128)S(1)}, u32[]{:S(2)}) copy-start(f32[2,3,180]{2,1,0:T(4,128)S(1)} %get-tuple-element.74) | copy-start | bytes 12964
  122.8 2.9 %slice-start.1 = ((s8[4521984]{0:T(1024)(128)(4,1)}), s8[327680]{0:T(1024)(128)(4,1)S(1)}, s32[]{:S(2)}) async-start(s8[4521984]{0:T(1024)(128)(4,1)} %bitcast.336), calls=%async_computation.10 | async-start | bytes 655360
  125.7 5.4 %copy-start.31 = (f32[2,3,180,1024]{3,2,1,0:T(8,128)}, f32[2,3,180,1024]{3,2,1,0:T(8,128)S(1)}, u32[]{:S(2)}) copy-start(f32[2,3,180,1024]{3,2,1,0:T(8,128)S(1)} %fusion.14) | copy-start | bytes 13271044
  131.2 90.8 %reduce-scatter.3.cloned.1.call-start = ((), (), s32[]{:S(2)}) async-start(), calls=%async_computation.7 | async-start | bytes 2826240 | tf_op jit(solution)/shard_map/reduce_scatter | solution.py:196
  138.2 5.3 %collective-permute-start.7 = (f32[2,2,3,180]{3,2,1,0:T(4,128)S(1)}, f32[2,2,3,180]{3,2,1,0:T(4,128)S(1)}, u32[]{:S(2)}, u32[]{:S(2)}) collective-permute-start(f32[2,2,3,180]{3,2,1,0:T(4,128)S(1)} %get-tuple-element.70), channel_id=1, source_target_pairs={{0,2},{1,3},{2,0},{3,1},{4,6},{5,7},{6,4},{7,5},{8,10},{9,11},{10,... | collective-permute-start | bytes 25928 | tf_op jit(solution)/shard_map/ppermute | solution.py:164
  140.9 4.0 %collective-permute-start.6 = (f32[2,2,3,180]{3,2,1,0:T(4,128)S(1)}, f32[2,2,3,180]{3,2,1,0:T(4,128)S(1)}, u32[]{:S(2)}, u32[]{:S(2)}) collective-permute-start(f32[2,2,3,180]{3,2,1,0:T(4,128)S(1)} %get-tuple-element.70), channel_id=1, source_target_pairs={{0,3},{1,0},{2,1},{3,2},{4,7},{5,4},{6,5},{7,6},{8,11},{9,8},{10,9... | collective-permute-start | bytes 25928 | tf_op jit(solution)/shard_map/ppermute | solution.py:164
  141.7 5.3 %collective-permute-start.8 = (f32[2,2,3,180]{3,2,1,0:T(4,128)S(1)}, f32[2,2,3,180]{3,2,1,0:T(4,128)S(1)}, u32[]{:S(2)}, u32[]{:S(2)}) collective-permute-start(f32[2,2,3,180]{3,2,1,0:T(4,128)S(1)} %get-tuple-element.70), channel_id=1, source_target_pairs={{0,1},{1,2},{2,3},{3,0},{4,5},{5,6},{6,7},{7,4},{8,9},{9,10},{10,1... | collective-permute-start | bytes 25928 | tf_op jit(solution)/shard_map/ppermute | solution.py:164
  189.6 2.1 copy-start.6
  193.4 17.1 %copy-start.16 = (bf16[2,3,180,256]{3,2,1,0:T(8,128)(2,1)S(1)}, bf16[2,3,180,256]{3,2,1,0:T(8,128)(2,1)}, u32[]{:S(2)}) copy-start(bf16[2,3,180,256]{3,2,1,0:T(8,128)(2,1)} %reduce-scatter.5.cloned.1.call-done) | copy-start | bytes 1658884
  194.0 16.5 %copy-start.4 = (bf16[2,3,180,256]{3,0,2,1:T(2,128)(2,1)S(1)}, bf16[2,3,180,256]{3,0,2,1:T(2,128)(2,1)}, u32[]{:S(2)}) copy-start(bf16[2,3,180,256]{3,0,2,1:T(2,128)(2,1)} %param.8) | copy-start | bytes 1658884
  194.0 16.5 %copy-start.8 = (bf16[2,3,180,256]{3,2,1,0:T(8,128)(2,1)S(1)}, bf16[2,3,180,256]{3,2,1,0:T(8,128)(2,1)}, u32[]{:S(2)}) copy-start(bf16[2,3,180,256]{3,2,1,0:T(8,128)(2,1)} %fusion.36) | copy-start | bytes 1658884
  194.0 16.5 %copy-start.12 = (bf16[2,3,180,256]{3,0,2,1:T(2,128)(2,1)S(1)}, bf16[2,3,180,256]{3,0,2,1:T(2,128)(2,1)}, u32[]{:S(2)}) copy-start(bf16[2,3,180,256]{3,0,2,1:T(2,128)(2,1)} %param.9) | copy-start | bytes 1658884
  194.0 16.4 %copy-start.15 = (f32[2,180,96]{2,1,0:T(8,128)S(1)}, f32[2,180,96]{2,1,0:T(8,128)}, u32[]{:S(2)}) copy-start(f32[2,180,96]{2,1,0:T(8,128)} %pad_maximum_fusion.2) | copy-start | bytes 414724
  194.0 16.4 %copy-start.24 = (f32[2,3,180]{2,1,0:T(4,128)S(1)}, f32[2,3,180]{2,1,0:T(4,128)}, u32[]{:S(2)}) copy-start(f32[2,3,180]{2,1,0:T(4,128)} %copy-done.23) | copy-start | bytes 12964
  194.0 16.4 %copy-start.26 = (f32[2,3,180]{2,1,0:T(4,128)S(1)}, f32[2,3,180]{2,1,0:T(4,128)}, u32[]{:S(2)}) copy-start(f32[2,3,180]{2,1,0:T(4,128)} %copy-done.25) | copy-start | bytes 12964
  210.5 11.5 %copy-start.9 = (bf16[2,3,180,256]{3,2,1,0:T(8,128)(2,1)S(1)}, bf16[2,3,180,256]{3,2,1,0:T(8,128)(2,1)}, u32[]{:S(2)}) copy-start(bf16[2,3,180,256]{3,2,1,0:T(8,128)(2,1)} %fusion.36) | copy-start | bytes 1658884
  213.3 5.3 %collective-permute-start.10 = (f32[2,2,3,180]{3,2,1,0:T(4,128)S(1)}, f32[2,2,3,180]{3,2,1,0:T(4,128)S(1)}, u32[]{:S(2)}, u32[]{:S(2)}) collective-permute-start(f32[2,2,3,180]{3,2,1,0:T(4,128)S(1)} %get-tuple-element.66), channel_id=1, source_target_pairs={{0,2},{1,3},{2,0},{3,1},{4,6},{5,7},{6,4},{7,5},{8,10},{9,11},{10,... | collective-permute-start | bytes 25928 | tf_op jit(solution)/shard_map/ppermute | solution.py:164
  214.6 4.0 %collective-permute-start.9 = (f32[2,2,3,180]{3,2,1,0:T(4,128)S(1)}, f32[2,2,3,180]{3,2,1,0:T(4,128)S(1)}, u32[]{:S(2)}, u32[]{:S(2)}) collective-permute-start(f32[2,2,3,180]{3,2,1,0:T(4,128)S(1)} %get-tuple-element.66), channel_id=1, source_target_pairs={{0,3},{1,0},{2,1},{3,2},{4,7},{5,4},{6,5},{7,6},{8,11},{9,8},{10,9... | collective-permute-start | bytes 25928 | tf_op jit(solution)/shard_map/ppermute | solution.py:164
  216.2 4.9 %collective-permute-start.11 = (f32[2,2,3,180]{3,2,1,0:T(4,128)S(1)}, f32[2,2,3,180]{3,2,1,0:T(4,128)S(1)}, u32[]{:S(2)}, u32[]{:S(2)}) collective-permute-start(f32[2,2,3,180]{3,2,1,0:T(4,128)S(1)} %get-tuple-element.66), channel_id=1, source_target_pairs={{0,1},{1,2},{2,3},{3,0},{4,5},{5,6},{6,7},{7,4},{8,9},{9,10},{10,1... | collective-permute-start | bytes 25928 | tf_op jit(solution)/shard_map/ppermute | solution.py:164
  (2 other events, 2.1 us)
Sparse Core Ops, SparseCore 0:
  88.5 31.7 all-gather.1
  131.3 32.2 reduce-scatter.4
  166.2 30.4 reduce-scatter.2
where the time goes:
time: 235 us; the launch traced here: 234 us
  waiting for transfers between devices  60.9 us (26%)
  blocking collectives  53.7 us (23%)
  matrix products  37.6 us (16%)
  local copies, waits for them, and re-layouts  25.4 us (11%)
  starting transfers between devices  25.2 us (11%)
  other arithmetic  16.9 us (7%)
  between operations  14.6 us (6%)
    all_to_all x2, blocking collectives, stacked_rows(): lax.all_to_all(field.astype(link_type), 'space', 2, 3, tiled=True)  34.9 us
    all_gather x1, waiting for transfers between devices, per_device(): whole_residual = lax.all_gather(residual, 'feat', axis=3, tiled=True)  22 us
    all_to_all x1, blocking collectives, stacked_columns(): lax.all_to_all(field.astype(link_type), 'space', 3, 2, tiled=True)  18.8 us
    all_to_all x1, waiting for transfers between devices, stacked_columns(): lax.all_to_all(field.astype(link_type), 'space', 3, 2, tiled=True)  15 us
    reduce_scatter x2, waiting for transfers between devices, channel_share(): lax.psum_scatter(term.astype(jnp.bfloat16), 'feat', scatter_dimension=3,...  14.4 us
    ppermute x9, starting transfers between devices, token_sums(): lax.ppermute(pair, 'feat', [(i, (i + count - shift) % count) for i in ran...  13.4 us
    ppermute x9, waiting for transfers between devices, token_sums(): lax.ppermute(pair, 'feat', [(i, (i + count - shift) % count) for i in ran...  8.58 us
    all_to_all x1, starting transfers between devices, stacked_columns(): lax.all_to_all(field.astype(link_type), 'space', 3, 2, tiled=True)  8.17 us
  transfers between devices with their start and end apart: 16, of which 9 were waited for; matrix products, arithmetic and copies ran while one was open for 21% of the time, Pallas kernels for 0%

commit v1 on v0

--- a/solution.py
+++ b/solution.py
@@ -243,7 +243,9 @@
     shrunk, cotangent_parts = lax.optimization_barrier((shrunk, cotangent_parts))
     whole_cotangent = ring_assemble(cotangent_parts)
     filtered = lon_stacked_back(
-        stacked_rows(lat_stacked(lat_inverse_op, shrunk), jnp.bfloat16), lon_inv_tables
+        stacked_rows(lat_stacked(lat_inverse_op, shrunk, lax.Precision.DEFAULT), jnp.bfloat16),
+        lon_inv_tables,
+        lax.Precision.DEFAULT,
     )
     residual = (filtered + normed + values).astype(jnp.bfloat16)
     residual_vals = residual.astype(jnp.float32)

time: 235 us -> 233 us (level)
    unnamed x70 -> x68, local copies, waits for them, and re-layouts: 5.35 us -> 5.52 us
where the time goes in v1:
time: 233 us; the launch traced here: 232 us
  waiting for transfers between devices  61 us (26%)
  blocking collectives  53.7 us (23%)
  matrix products  37.1 us (16%)
  local copies, waits for them, and re-layouts  25.5 us (11%)
  starting transfers between devices  25 us (11%)
  other arithmetic  15.5 us (7%)
  between operations  14.6 us (6%)
    all_to_all x2, blocking collectives, stacked_rows(): lax.all_to_all(field.astype(link_type), 'space', 2, 3, tiled=True)  34.9 us
    all_gather x1, waiting for transfers between devices, per_device(): whole_residual = lax.all_gather(residual, 'feat', axis=3, tiled=True)  22.2 us
    all_to_all x1, blocking collectives, stacked_columns(): lax.all_to_all(field.astype(link_type), 'space', 3, 2, tiled=True)  18.8 us
    all_to_all x1, waiting for transfers between devices, stacked_columns(): lax.all_to_all(field.astype(link_type), 'space', 3, 2, tiled=True)  15 us
    reduce_scatter x2, waiting for transfers between devices, channel_share(): lax.psum_scatter(term.astype(jnp.bfloat16), 'feat', scatter_dimension=3,...  14.4 us
    ppermute x9, starting transfers between devices, token_sums(): lax.ppermute(pair, 'feat', [(i, (i + count - shift) % count) for i in ran...  13.4 us
    ppermute x9, waiting for transfers between devices, token_sums(): lax.ppermute(pair, 'feat', [(i, (i + count - shift) % count) for i in ran...  8.57 us
    all_to_all x1, starting transfers between devices, stacked_columns(): lax.all_to_all(field.astype(link_type), 'space', 3, 2, tiled=True)  8.17 us
  transfers between devices with their start and end apart: 16, of which 9 were waited for; matrix products, arithmetic and copies ran while one was open for 21% of the time, Pallas kernels for 0%

profile of v1, /device:TPU:0, one launch (start us, length us, event | category | flops | bytes accessed | tf_op | source)
XLA Modules:
  0.0 232.3 jit_solution(46444339401300761)
XLA Ops:
  7.2 1.7 convert_reduce_fusion.1
  9.5 3.3 %collective-permute-start.1 = (f32[2,2,3,180]{3,2,1,0:T(4,128)}, f32[2,2,3,180]{3,2,1,0:T(4,128)}, u32[]{:S(2)}, u32[]{:S(2)}) collective-permute-start(f32[2,2,3,180]{3,2,1,0:T(4,128)} %get-tuple-element.70), channel_id=1, source_target_pairs={{0,2},{1,3},{2,0},{3,1},{4,6},{5,7},{6,4},{7,5},{8,10},{9,11},{10,... | collective-permute-start | bytes 25928 | tf_op jit(solution)/shard_map/ppermute | solution.py:164
  12.8 1.1 collective-permute-start
  13.8 1.0 collective-permute-start.2
  19.5 1.1 maximum_bitcast_fusion.1
  20.6 0.8 pad_maximum_fusion.8
  22.0 1.9 convolution_bitcast_fusion.7
  24.0 2.0 copy.105
  26.0 8.2 %all-to-all-start = ((f32[2,2,3,96,256]{4,1,2,0,3:T(2,128)}), f32[2,2,3,96,256]{4,1,2,0,3:T(2,128)S(1)}, u32[]{:S(2)}, u32[]{:S(2)}) async-start(f32[2,2,3,96,256]{4,1,2,0,3:T(2,128)} %copy.105), calls=%async_computation | async-start | bytes 2359296 | tf_op jit(solution)/shard_map/all_to_all | solution.py:150
  34.2 2.3 %collective-permute-start.5 = (bf16[2,3,180,256]{3,0,2,1:T(2,128)(2,1)}, bf16[2,3,180,256]{3,0,2,1:T(2,128)(2,1)}, u32[]{:S(2)}, u32[]{:S(2)}) collective-permute-start(bf16[2,3,180,256]{3,0,2,1:T(2,128)(2,1)} %param.9), channel_id=1, source_target_pairs={{0,3},{1,0},{2,1},{3,2},{4,7},{5,4},{6,5},{7,6},{8,11},{9,8},{10,9... | collective-permute-start | bytes 1658888 | tf_op jit(solution)/shard_map/ppermute | solution.py:178
  37.5 15.0 %all-to-all-done = f32[2,2,3,96,256]{4,1,2,0,3:T(2,128)S(1)} async-done(((f32[2,2,3,96,256]{4,1,2,0,3:T(2,128)}), f32[2,2,3,96,256]{4,1,2,0,3:T(2,128)S(1)}, u32[]{:S(2)}, u32[]{:S(2)}) %all-to-all-start) | async-done | bytes 1179680 | tf_op jit(solution)/shard_map/all_to_all | solution.py:150
  52.5 1.1 copy-done.5
  53.6 1.7 copy.107
  55.3 1.7 convolution_bitcast_fusion.6
  57.0 2.8 %reshape.280 = f32[2,2,96,3,2,128]{5,4,2,0,3,1:T(2,128)} reshape(f32[2,2,96,3,256]{4,2,0,3,1:T(8,128)} %convolution_bitcast_fusion.6) | data formatting | bytes 2359296 | tf_op jit(solution)/shard_map/reshape | solution.py:61
  59.8 2.1 fusion.30
  62.7 1.0 copy-done.1
  65.6 19.0 %all_to_all.72 = bf16[2,2,96,3,256]{4,0,3,1,2:T(2,128)(2,1)S(1)} all-to-all(bf16[2,2,96,3,256]{4,0,3,1,2:T(2,128)(2,1)S(1)} %copy.117), channel_id=1, replica_groups=mesh['space'=32,'feat'=4] {'space'}, dimensions={2} | all-to-all | bytes 1179648 | tf_op jit(solution)/shard_map/all_to_all | solution.py:154
  85.0 1.3 fusion.36
  87.6 1.2 copy_dynamic-update-slice_fusion.2
  88.8 1.3 copy_dynamic-update-slice_fusion.1
  90.1 1.2 copy_dynamic-update-slice_fusion
  91.3 4.7 %fusion.23 = f32[2,3,180,1024]{3,2,1,0:T(8,128)} fusion(bf16[2,3,180,1024]{3,2,1,0:T(8,128)(2,1)S(1)} %copy_dynamic-update-slice_fusion, bf16[1024,1024]{1,0:T(8,128)(2,1)S(1)} %copy-done.29), kind=kOutput, calls=%fused_computation.30 | convolution fusion | flops 2264924160 | bytes 8732672 | tf_op jit(solution)/shard_map/brwd,hd->brwh/dot_general | solution.py:253
  96.0 22.2 %all-gather.2.cloned.1.call-done = bf16[2,3,180,1024]{3,2,1,0:T(8,128)(2,1)} async-done(((bf16[2,3,180,256]{3,2,1,0:T(8,128)(2,1)}), bf16[2,3,180,1024]{3,2,1,0:T(8,128)(2,1)}) %all-gather.2.cloned.1.call-update) | async-done | bytes 2211856 | tf_op jit(solution)/shard_map/all_gather | solution.py:252
  118.3 2.5 %convert_reduce_fusion = (f32[2,3,180]{2,1,0:T(4,128)S(1)}, f32[2,3,180]{2,1,0:T(4,128)S(1)}) fusion(bf16[2,3,180,1024]{3,2,1,0:T(8,128)(2,1)} %all-gather.2.cloned.1.call-done), kind=kLoop, calls=%fused_computation.6 | loop fusion | flops 4421520 | bytes 2220480 | tf_op jit(solution)/shard_map/reduce_sum | solution.py:258
  120.9 2.8 %fusion.14 = f32[2,3,180,1024]{3,2,1,0:T(8,128)S(1)} fusion(bf16[2,3,180,1024]{3,2,1,0:T(8,128)(2,1)S(1)} %copy-done.10, f32[2,3,180]{2,1,0:T(4,128)S(1)} %get-tuple-element.72, f32[2,3,180]{2,1,0:T(4,128)S(1)} %get-tuple-element.71, bf16[1024,1024]{1,0:T(8,128)(2,1)S(1)} %copy-done), kind=kOutput, calls=%fused_computation.22 | convolution fusion | flops 2269347840 | bytes 8741312 | tf_op jit(solution)/shard_map/brwd,dh->brwh/dot_general | solution.py:262
  123.8 5.4 %fusion.127 = (f32[2,3,180]{2,1,0:T(4,128)S(1)}, f32[2,3,180]{2,1,0:T(4,128)S(1)}, bf16[2,3,180,1024]{3,2,1,0:T(8,128)(2,1)}) fusion(f32[2,3,180]{2,1,0:T(4,128)S(1)} %get-tuple-element.72, f32[2,3,180]{2,1,0:T(4,128)S(1)} %get-tuple-element.71, bf16[2,3,180,1024]{3,2,1,0:T(8,128)(2,1)S(1)} %copy-done.10, bf16[1024,1024]{1,0:T(8,128)(2,1)S(1)} %copy-done, ...), kind=kOutput, calls=%fused_computation.214 | convolution fusion | flops 2283722752 | bytes 15385472 | tf_op jit(solution)/shard_map/brwh,dh->brwd/dot_general | solution.py:271
  129.2 6.9 %fusion.27 = bf16[2,3,180,1024]{3,2,1,0:T(8,128)(2,1)} fusion(bf16[1024,1024]{1,0:T(8,128)(2,1)} %param.15, f32[2,3,180,1024]{3,2,1,0:T(8,128)} %copy-done.30), kind=kOutput, calls=%fused_computation.38 | convolution fusion | flops 2271559680 | bytes 8732672 | tf_op jit(solution)/shard_map/brwh,hd->brwd/dot_general | solution.py:266
  136.2 2.8 %collective-permute-start.7 = (f32[2,2,3,180]{3,2,1,0:T(4,128)S(1)}, f32[2,2,3,180]{3,2,1,0:T(4,128)S(1)}, u32[]{:S(2)}, u32[]{:S(2)}) collective-permute-start(f32[2,2,3,180]{3,2,1,0:T(4,128)S(1)} %get-tuple-element.68), channel_id=1, source_target_pairs={{0,2},{1,3},{2,0},{3,1},{4,6},{5,7},{6,4},{7,5},{8,10},{9,11},{10,... | collective-permute-start | bytes 25928 | tf_op jit(solution)/shard_map/ppermute | solution.py:164
  139.7 1.3 collective-permute-start.8
  141.5 1.5 collective-permute-done.6
  143.0 2.0 collective-permute-done.8
  145.7 1.5 gather_fusion.1
  147.2 14.4 %reduce-scatter.5.cloned.1.call-done = bf16[2,3,180,256]{3,2,1,0:T(8,128)(2,1)} async-done(((bf16[2,3,180,1024]{3,2,1,0:T(8,128)(2,1)}), bf16[2,3,180,256]{3,2,1,0:T(8,128)(2,1)}) %reduce-scatter.5.cloned.1.call-update) | async-done | bytes 552976 | tf_op jit(solution)/shard_map/reduce_scatter | solution.py:196
  161.6 2.4 %fusion.39 = bf16[2,2,3,96,256]{4,3,2,1,0:T(8,128)(2,1)S(1)} fusion(bf16[2,180,96]{2,1,0:T(8,128)(2,1)} %pad_maximum_fusion.3, bf16[2,3,180,256]{3,2,1,0:T(8,128)(2,1)} %fusion.36, bf16[2,3,180,256]{3,2,1,0:T(8,128)(2,1)} %reduce-scatter.5.cloned.1.call-done, bf16[2,3,180,256]{3,0,2,1:T(2,128)(2,1)} %param.9, f32[2,3,180]{2,1,0:T(4,128)S(1)} %get-tuple-element.66, ...), kind=kOutput, calls=%fused_computation.63 | convolution fusion | flops 108933120 | bytes 2335104 | tf_op jit(solution)/shard_map/brwc,pwk->pbrkc/dot_general | solution.py:130
  164.6 18.8 %all_to_all.73 = bf16[2,2,3,96,256]{4,1,2,0,3:T(2,128)(2,1)S(1)} all-to-all(bf16[2,2,3,96,256]{4,1,2,0,3:T(2,128)(2,1)S(1)} %copy.126), channel_id=1, replica_groups=mesh['space'=32,'feat'=4] {'space'}, dimensions={3} | all-to-all | bytes 1179648 | tf_op jit(solution)/shard_map/all_to_all | solution.py:150
  183.8 1.2 convolution_bitcast_fusion.8
  185.0 2.5 %reshape.338 = bf16[2,2,96,3,2,128]{5,4,2,0,3,1:T(2,128)(2,1)} reshape(bf16[2,2,96,3,256]{4,2,0,3,1:T(8,128)(2,1)} %convolution_bitcast_fusion.8) | data formatting | bytes 1179648 | tf_op jit(solution)/shard_map/reshape | solution.py:61
  187.6 2.1 fusion.38
  192.1 15.9 %all_to_all.74 = bf16[2,2,96,3,256]{4,0,3,1,2:T(2,128)(2,1)S(1)} all-to-all(bf16[2,2,96,3,256]{4,0,3,1,2:T(2,128)(2,1)S(1)} %copy.138), channel_id=1, replica_groups=mesh['space'=32,'feat'=4] {'space'}, dimensions={2} | all-to-all | bytes 1179648 | tf_op jit(solution)/shard_map/all_to_all | solution.py:154
  208.5 2.8 %fusion.128 = (f32[2,3,180]{2,1,0:T(4,128)S(1)}, f32[2,3,180]{2,1,0:T(4,128)S(1)}, f32[2,3,180,256]{3,2,1,0:T(8,128)}) fusion(f32[2,3,180]{2,1,0:T(4,128)S(1)} %fusion.114, f32[2,3,180]{2,1,0:T(4,128)S(1)} %fusion.115, bf16[2,3,180,256]{3,0,2,1:T(2,128)(2,1)S(1)} %copy-done.4, bf16[2,2,3,96,256]{4,1,3,2,0:T(2,128)(2,1)S(1)} %bitcast.302, ...), kind=kOutput, calls=%fused_computation.215 | convolution fusion | flops 110866320 | bytes 4080384 | tf_op jit(solution)/shard_map/pbrkc,pwk->brwc/dot_general | solution.py:134
  211.3 1.3 collective-permute-start.10
  212.6 1.6 collective-permute-start.9
  214.6 2.0 collective-permute-done.10
  216.6 2.5 %collective-permute-done.11 = f32[2,2,3,180]{3,2,1,0:T(4,128)S(1)} collective-permute-done((f32[2,2,3,180]{3,2,1,0:T(4,128)S(1)}, f32[2,2,3,180]{3,2,1,0:T(4,128)S(1)}, u32[]{:S(2)}, u32[]{:S(2)}) %collective-permute-start.11) | collective-permute-done | bytes 8672 | tf_op jit(solution)/shard_map/ppermute | solution.py:164
  220.0 3.4 %fusion.67 = (bf16[2,3,180,256]{3,2,1,0:T(8,128)(2,1)S(1)}, bf16[2,3,180,256]{3,2,1,0:T(8,128)(2,1)S(1)}) fusion(f32[2,3,180,256]{3,2,1,0:T(8,128)} %get-tuple-element.76, f32[2,3,180]{2,1,0:T(4,128)S(1)} %get-tuple-element.62, f32[2,3,180]{2,1,0:T(4,128)S(1)} %get-tuple-element.61, f32[2,3,180]{2,1,0:T(4,128)S(1)} %fusion.114, ...), kind=kLoop, calls=%fused_computation.94 | loop fusion | flops 6082560 | bytes 5011200 | tf_op jit(solution)/shard_map/convert_element_type | solution.py:309
  223.3 1.2 copy.143
  224.6 1.2 copy.142
  (134 shorter events, 18.0 us)
Async XLA Ops:
  7.2 113.7 %copy-start = (bf16[1024,1024]{1,0:T(8,128)(2,1)S(1)}, bf16[1024,1024]{1,0:T(8,128)(2,1)}, u32[]{:S(2)}) copy-start(bf16[1024,1024]{1,0:T(8,128)(2,1)} %param.14) | copy-start | bytes 6291460
  7.2 10.0 %copy-start.17 = (f32[2,2,128,128]{3,2,1,0:T(8,128)S(1)}, f32[2,2,128,128]{3,2,1,0:T(8,128)}, u32[]{:S(2)}) copy-start(f32[2,2,128,128]{3,2,1,0:T(8,128)} %param.10) | copy-start | bytes 786436
  7.2 10.1 %copy-start.18 = (f32[2,2,128,128]{3,2,1,0:T(8,128)S(1)}, f32[2,2,128,128]{3,2,1,0:T(8,128)}, u32[]{:S(2)}) copy-start(f32[2,2,128,128]{3,2,1,0:T(8,128)} %param.12) | copy-start | bytes 786436
  9.5 11.1 %collective-permute-start.1 = (f32[2,2,3,180]{3,2,1,0:T(4,128)}, f32[2,2,3,180]{3,2,1,0:T(4,128)}, u32[]{:S(2)}, u32[]{:S(2)}) collective-permute-start(f32[2,2,3,180]{3,2,1,0:T(4,128)} %get-tuple-element.70), channel_id=1, source_target_pairs={{0,2},{1,3},{2,0},{3,1},{4,6},{5,7},{6,4},{7,5},{8,10},{9,11},{10,... | collective-permute-start | bytes 25928 | tf_op jit(solution)/shard_map/ppermute | solution.py:164
  12.8 7.8 %collective-permute-start = (f32[2,2,3,180]{3,2,1,0:T(4,128)}, f32[2,2,3,180]{3,2,1,0:T(4,128)}, u32[]{:S(2)}, u32[]{:S(2)}) collective-permute-start(f32[2,2,3,180]{3,2,1,0:T(4,128)} %get-tuple-element.70), channel_id=1, source_target_pairs={{0,3},{1,0},{2,1},{3,2},{4,7},{5,4},{6,5},{7,6},{8,11},{9,8},{10,9... | collective-permute-start | bytes 25928 | tf_op jit(solution)/shard_map/ppermute | solution.py:164
  13.8 6.8 %collective-permute-start.2 = (f32[2,2,3,180]{3,2,1,0:T(4,128)}, f32[2,2,3,180]{3,2,1,0:T(4,128)}, u32[]{:S(2)}, u32[]{:S(2)}) collective-permute-start(f32[2,2,3,180]{3,2,1,0:T(4,128)} %get-tuple-element.70), channel_id=1, source_target_pairs={{0,1},{1,2},{2,3},{3,0},{4,5},{5,6},{6,7},{7,4},{8,9},{9,10},{10,1... | collective-permute-start | bytes 25928 | tf_op jit(solution)/shard_map/ppermute | solution.py:164
  17.2 1.5 copy-start.19
  17.2 1.5 copy-start.20
  19.5 2.5 %copy-start.2 = (bf16[2,3,180,256]{3,0,2,1:T(2,128)(2,1)S(1)}, bf16[2,3,180,256]{3,0,2,1:T(2,128)(2,1)}, u32[]{:S(2)}) copy-start(bf16[2,3,180,256]{3,0,2,1:T(2,128)(2,1)} %param.8) | copy-start | bytes 1658884
  20.6 5.4 %copy-start.26 = (s32[1024]{0:T(1024)}, s32[1024]{0:T(1024)S(1)}, u32[]{:S(2)}) copy-start(s32[1024]{0:T(1024)S(1)} %pad_clamp_fusion) | copy-start | bytes 12292
  26.0 26.5 %all-to-all-start = ((f32[2,2,3,96,256]{4,1,2,0,3:T(2,128)}), f32[2,2,3,96,256]{4,1,2,0,3:T(2,128)S(1)}, u32[]{:S(2)}, u32[]{:S(2)}) async-start(f32[2,2,3,96,256]{4,1,2,0,3:T(2,128)} %copy.105), calls=%async_computation | async-start | bytes 2359296 | tf_op jit(solution)/shard_map/all_to_all | solution.py:150
  34.2 84.1 %all-gather.2.cloned.1.call-start = ((), (), s32[]{:S(2)}) async-start(), calls=%async_computation.6 | async-start | bytes 2826240 | tf_op jit(solution)/shard_map/all_gather | solution.py:252
  34.2 29.6 %collective-permute-start.5 = (bf16[2,3,180,256]{3,0,2,1:T(2,128)(2,1)}, bf16[2,3,180,256]{3,0,2,1:T(2,128)(2,1)}, u32[]{:S(2)}, u32[]{:S(2)}) collective-permute-start(bf16[2,3,180,256]{3,0,2,1:T(2,128)(2,1)} %param.9), channel_id=1, source_target_pairs={{0,3},{1,0},{2,1},{3,2},{4,7},{5,4},{6,5},{7,6},{8,11},{9,8},{10,9... | collective-permute-start | bytes 1658888 | tf_op jit(solution)/shard_map/ppermute | solution.py:178
  36.5 27.3 %collective-permute-start.4 = (bf16[2,3,180,256]{3,0,2,1:T(2,128)(2,1)}, bf16[2,3,180,256]{3,0,2,1:T(2,128)(2,1)}, u32[]{:S(2)}, u32[]{:S(2)}) collective-permute-start(bf16[2,3,180,256]{3,0,2,1:T(2,128)(2,1)} %param.9), channel_id=1, source_target_pairs={{0,2},{1,3},{2,0},{3,1},{4,6},{5,7},{6,4},{7,5},{8,10},{9,11},{10,... | collective-permute-start | bytes 1658888 | tf_op jit(solution)/shard_map/ppermute | solution.py:178
  37.0 27.5 %collective-permute-start.3 = (bf16[2,3,180,256]{3,0,2,1:T(2,128)(2,1)}, bf16[2,3,180,256]{3,0,2,1:T(2,128)(2,1)}, u32[]{:S(2)}, u32[]{:S(2)}) collective-permute-start(bf16[2,3,180,256]{3,0,2,1:T(2,128)(2,1)} %param.9), channel_id=1, source_target_pairs={{0,1},{1,2},{2,3},{3,0},{4,5},{5,6},{6,7},{7,4},{8,9},{9,10},{10,1... | collective-permute-start | bytes 1658888 | tf_op jit(solution)/shard_map/ppermute | solution.py:178
  52.5 1.1 copy-start.5
  57.0 2.8 %copy-start.27 = (f32[2,256]{1,0:T(2,128)S(1)}, f32[2,256]{1,0:T(2,128)}, u32[]{:S(2)}) copy-start(f32[2,256]{1,0:T(2,128)} %param.11) | copy-start | bytes 6148
  59.8 2.1 copy-start.7
  59.8 2.1 copy-start.28
  62.7 1.1 copy-start.1
  65.6 19.4 %copy-start.3 = (bf16[2,3,180,256]{3,0,2,1:T(2,128)(2,1)S(1)}, bf16[2,3,180,256]{3,0,2,1:T(2,128)(2,1)}, u32[]{:S(2)}) copy-start(bf16[2,3,180,256]{3,0,2,1:T(2,128)(2,1)} %param.8) | copy-start | bytes 1658884
  65.6 19.4 %copy-start.21 = (bf16[2,180,96]{2,1,0:T(8,128)(2,1)S(1)}, bf16[2,180,96]{2,1,0:T(8,128)(2,1)}, u32[]{:S(2)}) copy-start(bf16[2,180,96]{2,1,0:T(8,128)(2,1)} %pad_maximum_fusion.3) | copy-start | bytes 207364
  86.4 75.2 %reduce-scatter.5.cloned.1.call-start = ((), (), s32[]{:S(2)}) async-start(), calls=%async_computation.8 | async-start | bytes 2826240 | tf_op jit(solution)/shard_map/reduce_scatter | solution.py:196
  86.5 1.1 copy-start.11
  88.8 2.5 %copy-start.29 = (bf16[1024,1024]{1,0:T(8,128)(2,1)S(1)}, bf16[1024,1024]{1,0:T(8,128)(2,1)}, u32[]{:S(2)}) copy-start(bf16[1024,1024]{1,0:T(8,128)(2,1)} %param.15) | copy-start | bytes 6291460
  118.3 2.6 %copy-start.10 = (bf16[2,3,180,1024]{3,2,1,0:T(8,128)(2,1)S(1)}, bf16[2,3,180,1024]{3,2,1,0:T(8,128)(2,1)}, u32[]{:S(2)}) copy-start(bf16[2,3,180,1024]{3,2,1,0:T(8,128)(2,1)} %all-gather.2.cloned.1.call-done) | copy-start | bytes 6635524
  118.3 5.5 %slice-start = ((s8[4521984]{0:T(1024)(128)(4,1)}), s8[4194304]{0:T(1024)(128)(4,1)S(1)}, s32[]{:S(2)}) async-start(s8[4521984]{0:T(1024)(128)(4,1)} %bitcast.318), calls=%async_computation.9 | async-start | bytes 8388608
  120.8 2.9 %copy-start.22 = (f32[2,3,180]{2,1,0:T(4,128)}, f32[2,3,180]{2,1,0:T(4,128)S(1)}, u32[]{:S(2)}) copy-start(f32[2,3,180]{2,1,0:T(4,128)S(1)} %get-tuple-element.71) | copy-start | bytes 12964
  120.8 2.9 %copy-start.24 = (f32[2,3,180]{2,1,0:T(4,128)}, f32[2,3,180]{2,1,0:T(4,128)S(1)}, u32[]{:S(2)}) copy-start(f32[2,3,180]{2,1,0:T(4,128)S(1)} %get-tuple-element.72) | copy-start | bytes 12964
  120.9 2.9 %slice-start.1 = ((s8[4521984]{0:T(1024)(128)(4,1)}), s8[327680]{0:T(1024)(128)(4,1)S(1)}, s32[]{:S(2)}) async-start(s8[4521984]{0:T(1024)(128)(4,1)} %bitcast.318), calls=%async_computation.10 | async-start | bytes 655360
  123.8 5.4 %copy-start.30 = (f32[2,3,180,1024]{3,2,1,0:T(8,128)}, f32[2,3,180,1024]{3,2,1,0:T(8,128)S(1)}, u32[]{:S(2)}) copy-start(f32[2,3,180,1024]{3,2,1,0:T(8,128)S(1)} %fusion.14) | copy-start | bytes 13271044
  129.2 90.8 %reduce-scatter.3.cloned.1.call-start = ((), (), s32[]{:S(2)}) async-start(), calls=%async_computation.7 | async-start | bytes 2826240 | tf_op jit(solution)/shard_map/reduce_scatter | solution.py:196
  136.2 5.3 %collective-permute-start.7 = (f32[2,2,3,180]{3,2,1,0:T(4,128)S(1)}, f32[2,2,3,180]{3,2,1,0:T(4,128)S(1)}, u32[]{:S(2)}, u32[]{:S(2)}) collective-permute-start(f32[2,2,3,180]{3,2,1,0:T(4,128)S(1)} %get-tuple-element.68), channel_id=1, source_target_pairs={{0,2},{1,3},{2,0},{3,1},{4,6},{5,7},{6,4},{7,5},{8,10},{9,11},{10,... | collective-permute-start | bytes 25928 | tf_op jit(solution)/shard_map/ppermute | solution.py:164
  139.0 4.0 %collective-permute-start.6 = (f32[2,2,3,180]{3,2,1,0:T(4,128)S(1)}, f32[2,2,3,180]{3,2,1,0:T(4,128)S(1)}, u32[]{:S(2)}, u32[]{:S(2)}) collective-permute-start(f32[2,2,3,180]{3,2,1,0:T(4,128)S(1)} %get-tuple-element.68), channel_id=1, source_target_pairs={{0,3},{1,0},{2,1},{3,2},{4,7},{5,4},{6,5},{7,6},{8,11},{9,8},{10,9... | collective-permute-start | bytes 25928 | tf_op jit(solution)/shard_map/ppermute | solution.py:164
  139.7 5.3 %collective-permute-start.8 = (f32[2,2,3,180]{3,2,1,0:T(4,128)S(1)}, f32[2,2,3,180]{3,2,1,0:T(4,128)S(1)}, u32[]{:S(2)}, u32[]{:S(2)}) collective-permute-start(f32[2,2,3,180]{3,2,1,0:T(4,128)S(1)} %get-tuple-element.68), channel_id=1, source_target_pairs={{0,1},{1,2},{2,3},{3,0},{4,5},{5,6},{6,7},{7,4},{8,9},{9,10},{10,1... | collective-permute-start | bytes 25928 | tf_op jit(solution)/shard_map/ppermute | solution.py:164
  187.6 2.1 copy-start.6
  190.0 1.0 copy-start.14
  191.4 17.1 %copy-start.16 = (bf16[2,3,180,256]{3,2,1,0:T(8,128)(2,1)S(1)}, bf16[2,3,180,256]{3,2,1,0:T(8,128)(2,1)}, u32[]{:S(2)}) copy-start(bf16[2,3,180,256]{3,2,1,0:T(8,128)(2,1)} %reduce-scatter.5.cloned.1.call-done) | copy-start | bytes 1658884
  192.0 16.5 %copy-start.4 = (bf16[2,3,180,256]{3,0,2,1:T(2,128)(2,1)S(1)}, bf16[2,3,180,256]{3,0,2,1:T(2,128)(2,1)}, u32[]{:S(2)}) copy-start(bf16[2,3,180,256]{3,0,2,1:T(2,128)(2,1)} %param.8) | copy-start | bytes 1658884
  192.0 16.4 %copy-start.8 = (bf16[2,3,180,256]{3,2,1,0:T(8,128)(2,1)S(1)}, bf16[2,3,180,256]{3,2,1,0:T(8,128)(2,1)}, u32[]{:S(2)}) copy-start(bf16[2,3,180,256]{3,2,1,0:T(8,128)(2,1)} %fusion.36) | copy-start | bytes 1658884
  192.0 16.4 %copy-start.12 = (bf16[2,3,180,256]{3,0,2,1:T(2,128)(2,1)S(1)}, bf16[2,3,180,256]{3,0,2,1:T(2,128)(2,1)}, u32[]{:S(2)}) copy-start(bf16[2,3,180,256]{3,0,2,1:T(2,128)(2,1)} %param.9) | copy-start | bytes 1658884
  192.0 16.4 %copy-start.15 = (f32[2,180,96]{2,1,0:T(8,128)S(1)}, f32[2,180,96]{2,1,0:T(8,128)}, u32[]{:S(2)}) copy-start(f32[2,180,96]{2,1,0:T(8,128)} %pad_maximum_fusion.2) | copy-start | bytes 414724
  192.0 16.4 %copy-start.23 = (f32[2,3,180]{2,1,0:T(4,128)S(1)}, f32[2,3,180]{2,1,0:T(4,128)}, u32[]{:S(2)}) copy-start(f32[2,3,180]{2,1,0:T(4,128)} %copy-done.22) | copy-start | bytes 12964
  192.0 16.4 %copy-start.25 = (f32[2,3,180]{2,1,0:T(4,128)S(1)}, f32[2,3,180]{2,1,0:T(4,128)}, u32[]{:S(2)}) copy-start(f32[2,3,180]{2,1,0:T(4,128)} %copy-done.24) | copy-start | bytes 12964
  208.5 11.5 %copy-start.9 = (bf16[2,3,180,256]{3,2,1,0:T(8,128)(2,1)S(1)}, bf16[2,3,180,256]{3,2,1,0:T(8,128)(2,1)}, u32[]{:S(2)}) copy-start(bf16[2,3,180,256]{3,2,1,0:T(8,128)(2,1)} %fusion.36) | copy-start | bytes 1658884
  211.3 5.3 %collective-permute-start.10 = (f32[2,2,3,180]{3,2,1,0:T(4,128)S(1)}, f32[2,2,3,180]{3,2,1,0:T(4,128)S(1)}, u32[]{:S(2)}, u32[]{:S(2)}) collective-permute-start(f32[2,2,3,180]{3,2,1,0:T(4,128)S(1)} %get-tuple-element.64), channel_id=1, source_target_pairs={{0,2},{1,3},{2,0},{3,1},{4,6},{5,7},{6,4},{7,5},{8,10},{9,11},{10,... | collective-permute-start | bytes 25928 | tf_op jit(solution)/shard_map/ppermute | solution.py:164
  212.6 4.0 %collective-permute-start.9 = (f32[2,2,3,180]{3,2,1,0:T(4,128)S(1)}, f32[2,2,3,180]{3,2,1,0:T(4,128)S(1)}, u32[]{:S(2)}, u32[]{:S(2)}) collective-permute-start(f32[2,2,3,180]{3,2,1,0:T(4,128)S(1)} %get-tuple-element.64), channel_id=1, source_target_pairs={{0,3},{1,0},{2,1},{3,2},{4,7},{5,4},{6,5},{7,6},{8,11},{9,8},{10,9... | collective-permute-start | bytes 25928 | tf_op jit(solution)/shard_map/ppermute | solution.py:164
  214.2 4.9 %collective-permute-start.11 = (f32[2,2,3,180]{3,2,1,0:T(4,128)S(1)}, f32[2,2,3,180]{3,2,1,0:T(4,128)S(1)}, u32[]{:S(2)}, u32[]{:S(2)}) collective-permute-start(f32[2,2,3,180]{3,2,1,0:T(4,128)S(1)} %get-tuple-element.64), channel_id=1, source_target_pairs={{0,1},{1,2},{2,3},{3,0},{4,5},{5,6},{6,7},{7,4},{8,9},{9,10},{10,1... | collective-permute-start | bytes 25928 | tf_op jit(solution)/shard_map/ppermute | solution.py:164
  (1 other events, 0.9 us)
Sparse Core Ops, SparseCore 0:
  86.5 31.7 all-gather.1
  129.3 32.2 reduce-scatter.4
  164.2 30.4 reduce-scatter.2

commit v2 on v1

--- a/solution.py
+++ b/solution.py
@@ -226,7 +226,7 @@
     operators = lax.optimization_barrier(operators)
     lon_fwd_tables, lon_inv_tables, lat_forward_op, lat_inverse_op, first_op, second_op = operators
     values = inputs.astype(jnp.float32)
-    cotangent_parts = ring_send(cotangent)
+    cotangent_parts = lax.all_gather(cotangent, "feat", axis=3, tiled=True)
     first_sum, second_sum = token_sums(jnp.sum(values, axis=-1), jnp.sum(values * values, axis=-1))
     mean_one = first_sum[..., None] / full_width
     rstd_one = lax.rsqrt(second_sum[..., None] / full_width - mean_one * mean_one + EPSILON)
@@ -241,7 +241,7 @@
     second = block_stacked(first, second_op) + bias_two
     shrunk = (second - jnp.clip(second, -SHRINK_LEVEL, SHRINK_LEVEL)).reshape(spec.shape)
     shrunk, cotangent_parts = lax.optimization_barrier((shrunk, cotangent_parts))
-    whole_cotangent = ring_assemble(cotangent_parts)
+    whole_cotangent = cotangent_parts
     filtered = lon_stacked_back(
         stacked_rows(lat_stacked(lat_inverse_op, shrunk, lax.Precision.DEFAULT), jnp.bfloat16),
         lon_inv_tables,

time: 233 us -> 225 us (0.966)
  blocking collectives: 53.7 us -> 77.2 us
  waiting for transfers between devices: 61 us -> 49.5 us
  starting transfers between devices: 25 us -> 13.7 us
  local copies, waits for them, and re-layouts: 25.5 us -> 16 us
    all_to_all x1 -> x2, blocking collectives: 18.8 us -> 45.9 us  [stacked_columns(): lax.all_to_all(field.astype(link_type), 'space', 3, 2, tiled=True)]
    all_to_all x1 -> x0, waiting for transfers between devices: 15 us -> none  [stacked_columns(): lax.all_to_all(field.astype(link_type), 'space', 3, 2, tiled=True)]
    all_to_all x1 -> x0, starting transfers between devices: 8.17 us -> none  [stacked_columns(): lax.all_to_all(field.astype(link_type), 'space', 3, 2, tiled=True)]
    all_gather x1, waiting for transfers between devices: 22.2 us -> 26.5 us  [per_device(): whole_residual = lax.all_gather(residual, 'feat', axis=3, tiled=True)]
    dynamic_update_slice x4 -> x0, local copies, waits for them, and re-layouts: 3.76 us -> none  [ring_assemble(): lax.dynamic_update_slice_in_dim(whole, moved, source * width, axis=block....]
    all_to_all x2, blocking collectives: 34.9 us -> 31.3 us  [stacked_rows(): lax.all_to_all(field.astype(link_type), 'space', 2, 3, tiled=True)]
    ppermute x3 -> x0, starting transfers between devices: 3.28 us -> none  [ring_send(): lax.ppermute(block, 'feat', [(i, (i + shift) % count) for i in range(coun...]
    unnamed x68 -> x54, local copies, waits for them, and re-layouts: 5.52 us -> 3.6 us
  transfers between devices with their start and end apart: 16 -> 13, of which waited for: 9 -> 7; matrix products, arithmetic and copies ran while one was open for 21% -> 21% of each run, Pallas kernels for 0% -> 0%
where the time goes in v2:
time: 225 us; the launch traced here: 224 us
  blocking collectives  77.2 us (34%)
  waiting for transfers between devices  49.5 us (22%)
  matrix products  39.3 us (17%)
  local copies, waits for them, and re-layouts  16 us (7%)
  between operations  14.5 us (6%)
  other arithmetic  14.3 us (6%)
  starting transfers between devices  13.7 us (6%)
    all_to_all x2, blocking collectives, stacked_columns(): lax.all_to_all(field.astype(link_type), 'space', 3, 2, tiled=True)  45.9 us
    all_to_all x2, blocking collectives, stacked_rows(): lax.all_to_all(field.astype(link_type), 'space', 2, 3, tiled=True)  31.3 us
    all_gather x1, waiting for transfers between devices, per_device(): whole_residual = lax.all_gather(residual, 'feat', axis=3, tiled=True)  26.5 us
    reduce_scatter x2, waiting for transfers between devices, channel_share(): lax.psum_scatter(term.astype(jnp.bfloat16), 'feat', scatter_dimension=3,...  14.4 us
    ppermute x9, starting transfers between devices, token_sums(): lax.ppermute(pair, 'feat', [(i, (i + count - shift) % count) for i in ran...  13.5 us
    ppermute x9, waiting for transfers between devices, token_sums(): lax.ppermute(pair, 'feat', [(i, (i + count - shift) % count) for i in ran...  8.56 us
    dot_general x1, matrix products, per_device(): jnp.einsum('brwd,hd->brwh', whole_cotangent, down_weight, preferred_eleme...  6.92 us
    dot_general x1, matrix products, per_device(): jnp.einsum('brwh,hd->brwd', activated, down_weight, preferred_element_typ...  6.9 us
  transfers between devices with their start and end apart: 13, of which 7 were waited for; matrix products, arithmetic and copies ran while one was open for 21% of the time, Pallas kernels for 0%

profile of v2, /device:TPU:0, one launch (start us, length us, event | category | flops | bytes accessed | tf_op | source)
XLA Modules:
  0.0 224.5 jit_solution(13623127012717157272)
XLA Ops:
  7.2 1.7 convert_reduce_fusion.1
  9.0 3.4 %collective-permute-start.1 = (f32[2,2,3,180]{3,2,1,0:T(4,128)S(1)}, f32[2,2,3,180]{3,2,1,0:T(4,128)S(1)}, u32[]{:S(2)}, u32[]{:S(2)}) collective-permute-start(f32[2,2,3,180]{3,2,1,0:T(4,128)S(1)} %get-tuple-element.64), channel_id=1, source_target_pairs={{0,2},{1,3},{2,0},{3,1},{4,6},{5,7},{6,4},{7,5},{8,10},{9,11},{10,... | collective-permute-start | bytes 25928 | tf_op jit(solution)/shard_map/ppermute | solution.py:164
  12.3 1.1 collective-permute-start
  13.4 1.0 collective-permute-start.2
  16.3 0.6 pad_maximum_fusion.3
  17.0 0.7 pad_maximum_fusion.2
  17.7 0.7 pad_maximum_fusion.1
  18.4 1.1 maximum_bitcast_fusion.1
  20.2 1.9 convolution_bitcast_fusion.7
  22.2 0.9 copy.96
  23.1 27.1 %all_to_all.72 = f32[2,2,3,96,256]{4,1,2,0,3:T(2,128)S(1)} all-to-all(f32[2,2,3,96,256]{4,1,2,0,3:T(2,128)S(1)} %copy.96), channel_id=1, replica_groups=mesh['space'=32,'feat'=4] {'space'}, dimensions={3} | all-to-all | bytes 2359296 | tf_op jit(solution)/shard_map/all_to_all | solution.py:150
  50.6 0.7 convolution_bitcast_fusion.6
  51.3 1.6 reshape.280
  52.9 2.1 fusion.31
  55.0 0.7 fusion.32
  55.7 1.0 copy-done.1
  56.7 1.0 copy_bitcast_fusion
  57.7 1.4 fusion.42
  59.8 15.4 %all_to_all.73 = bf16[2,2,96,3,256]{4,0,3,1,2:T(2,128)(2,1)S(1)} all-to-all(bf16[2,2,96,3,256]{4,0,3,1,2:T(2,128)(2,1)S(1)} %copy.108), channel_id=1, replica_groups=mesh['space'=32,'feat'=4] {'space'}, dimensions={2} | all-to-all | bytes 1179648 | tf_op jit(solution)/shard_map/all_to_all | solution.py:154
  75.6 1.3 fusion.37
  77.0 6.9 %fusion.16 = f32[2,3,180,1024]{3,2,1,0:T(8,128)} fusion(bf16[2,3,180,1024]{3,0,2,1:T(2,128)(2,1)} %all-gather.3.cloned.1.call-done, bf16[1024,1024]{1,0:T(8,128)(2,1)} %param.15), kind=kOutput, calls=%fused_computation.23 | convolution fusion | flops 2264924160 | bytes 8732672 | tf_op jit(solution)/shard_map/brwd,hd->brwh/dot_general | solution.py:253
  83.9 26.5 %all-gather.5.cloned.1.call-done = bf16[2,3,180,1024]{3,2,1,0:T(8,128)(2,1)} async-done(((bf16[2,3,180,256]{3,2,1,0:T(8,128)(2,1)}), bf16[2,3,180,1024]{3,2,1,0:T(8,128)(2,1)}) %all-gather.5.cloned.1.call-update) | async-done | bytes 2211856 | tf_op jit(solution)/shard_map/all_gather | solution.py:252
  110.4 2.5 %convert_reduce_fusion = (f32[2,3,180]{2,1,0:T(4,128)S(1)}, f32[2,3,180]{2,1,0:T(4,128)S(1)}) fusion(bf16[2,3,180,1024]{3,2,1,0:T(8,128)(2,1)} %all-gather.5.cloned.1.call-done), kind=kLoop, calls=%fused_computation.6 | loop fusion | flops 4421520 | bytes 2220480 | tf_op jit(solution)/shard_map/reduce_sum | solution.py:258
  113.0 2.8 %fusion.14 = f32[2,3,180,1024]{3,2,1,0:T(8,128)S(1)} fusion(bf16[2,3,180,1024]{3,2,1,0:T(8,128)(2,1)S(1)} %copy-done.8, f32[2,3,180]{2,1,0:T(4,128)S(1)} %get-tuple-element.66, f32[2,3,180]{2,1,0:T(4,128)S(1)} %get-tuple-element.65, bf16[1024,1024]{1,0:T(8,128)(2,1)S(1)} %copy-done), kind=kOutput, calls=%fused_computation.22 | convolution fusion | flops 2269347840 | bytes 8741312 | tf_op jit(solution)/shard_map/brwd,dh->brwh/dot_general | solution.py:262
  115.9 5.4 %fusion.128 = (f32[2,3,180]{2,1,0:T(4,128)S(1)}, f32[2,3,180]{2,1,0:T(4,128)S(1)}, bf16[2,3,180,1024]{3,2,1,0:T(8,128)(2,1)}) fusion(f32[2,3,180]{2,1,0:T(4,128)S(1)} %get-tuple-element.66, f32[2,3,180]{2,1,0:T(4,128)S(1)} %get-tuple-element.65, bf16[2,3,180,1024]{3,2,1,0:T(8,128)(2,1)S(1)} %copy-done.8, bf16[1024,1024]{1,0:T(8,128)(2,1)S(1)} %copy-done, ...), kind=kOutput, calls=%fused_computation.211 | convolution fusion | flops 2283722752 | bytes 15385472 | tf_op jit(solution)/shard_map/brwh,dh->brwd/dot_general | solution.py:271
  121.4 6.9 %fusion.28 = bf16[2,3,180,1024]{3,2,1,0:T(8,128)(2,1)} fusion(bf16[1024,1024]{1,0:T(8,128)(2,1)} %param.15, f32[2,3,180,1024]{3,2,1,0:T(8,128)} %copy-done.23), kind=kOutput, calls=%fused_computation.39 | convolution fusion | flops 2271559680 | bytes 8732672 | tf_op jit(solution)/shard_map/brwh,hd->brwd/dot_general | solution.py:266
  128.4 2.8 %collective-permute-start.4 = (f32[2,2,3,180]{3,2,1,0:T(4,128)S(1)}, f32[2,2,3,180]{3,2,1,0:T(4,128)S(1)}, u32[]{:S(2)}, u32[]{:S(2)}) collective-permute-start(f32[2,2,3,180]{3,2,1,0:T(4,128)S(1)} %get-tuple-element.62), channel_id=1, source_target_pairs={{0,2},{1,3},{2,0},{3,1},{4,6},{5,7},{6,4},{7,5},{8,10},{9,11},{10,... | collective-permute-start | bytes 25928 | tf_op jit(solution)/shard_map/ppermute | solution.py:164
  131.1 0.8 collective-permute-start.3
  131.9 1.3 collective-permute-start.5
  133.7 1.4 collective-permute-done.3
  135.1 2.1 collective-permute-done.5
  137.8 1.5 gather_fusion.1
  139.4 14.4 %reduce-scatter.5.cloned.1.call-done = bf16[2,3,180,256]{3,2,1,0:T(8,128)(2,1)} async-done(((bf16[2,3,180,1024]{3,2,1,0:T(8,128)(2,1)}), bf16[2,3,180,256]{3,2,1,0:T(8,128)(2,1)}) %reduce-scatter.5.cloned.1.call-update) | async-done | bytes 552976 | tf_op jit(solution)/shard_map/reduce_scatter | solution.py:196
  153.8 2.4 %fusion.40 = bf16[2,2,3,96,256]{4,3,2,1,0:T(8,128)(2,1)S(1)} fusion(bf16[2,180,96]{2,1,0:T(8,128)(2,1)} %pad_maximum_fusion.3, bf16[2,3,180,256]{3,2,1,0:T(8,128)(2,1)} %fusion.37, bf16[2,3,180,256]{3,2,1,0:T(8,128)(2,1)} %reduce-scatter.5.cloned.1.call-done, bf16[2,3,180,256]{3,0,2,1:T(2,128)(2,1)} %param.9, f32[2,3,180]{2,1,0:T(4,128)S(1)} %get-tuple-element.60, ...), kind=kOutput, calls=%fused_computation.64 | convolution fusion | flops 108933120 | bytes 2335104 | tf_op jit(solution)/shard_map/brwc,pwk->pbrkc/dot_general | solution.py:130
  156.7 18.8 %all_to_all.74 = bf16[2,2,3,96,256]{4,1,2,0,3:T(2,128)(2,1)S(1)} all-to-all(bf16[2,2,3,96,256]{4,1,2,0,3:T(2,128)(2,1)S(1)} %copy.114), channel_id=1, replica_groups=mesh['space'=32,'feat'=4] {'space'}, dimensions={3} | all-to-all | bytes 1179648 | tf_op jit(solution)/shard_map/all_to_all | solution.py:150
  176.0 1.2 convolution_bitcast_fusion.8
  177.2 2.5 %reshape.338 = bf16[2,2,96,3,2,128]{5,4,2,0,3,1:T(2,128)(2,1)} reshape(bf16[2,2,96,3,256]{4,2,0,3,1:T(8,128)(2,1)} %convolution_bitcast_fusion.8) | data formatting | bytes 1179648 | tf_op jit(solution)/shard_map/reshape | solution.py:61
  179.7 2.1 fusion.39
  184.2 15.9 %all_to_all.75 = bf16[2,2,96,3,256]{4,0,3,1,2:T(2,128)(2,1)S(1)} all-to-all(bf16[2,2,96,3,256]{4,0,3,1,2:T(2,128)(2,1)S(1)} %copy.126), channel_id=1, replica_groups=mesh['space'=32,'feat'=4] {'space'}, dimensions={2} | all-to-all | bytes 1179648 | tf_op jit(solution)/shard_map/all_to_all | solution.py:154
  200.7 2.7 %fusion.129 = (f32[2,3,180]{2,1,0:T(4,128)S(1)}, f32[2,3,180]{2,1,0:T(4,128)S(1)}, f32[2,3,180,256]{3,2,1,0:T(8,128)}) fusion(f32[2,3,180]{2,1,0:T(4,128)S(1)} %fusion.115, f32[2,3,180]{2,1,0:T(4,128)S(1)} %fusion.116, bf16[2,3,180,256]{3,0,2,1:T(2,128)(2,1)S(1)} %copy-done.4, bf16[2,2,3,96,256]{4,1,3,2,0:T(2,128)(2,1)S(1)} %bitcast.301, ...), kind=kOutput, calls=%fused_computation.212 | convolution fusion | flops 110866320 | bytes 4080384 | tf_op jit(solution)/shard_map/pbrkc,pwk->brwc/dot_general | solution.py:134
  203.4 1.3 collective-permute-start.7
  204.7 1.6 collective-permute-start.6
  206.7 2.0 collective-permute-done.7
  208.7 2.6 %collective-permute-done.8 = f32[2,2,3,180]{3,2,1,0:T(4,128)S(1)} collective-permute-done((f32[2,2,3,180]{3,2,1,0:T(4,128)S(1)}, f32[2,2,3,180]{3,2,1,0:T(4,128)S(1)}, u32[]{:S(2)}, u32[]{:S(2)}) %collective-permute-start.8) | collective-permute-done | bytes 8672 | tf_op jit(solution)/shard_map/ppermute | solution.py:164
  211.3 0.7 gather_fusion.2
  212.1 3.4 %fusion.68 = (bf16[2,3,180,256]{3,2,1,0:T(8,128)(2,1)S(1)}, bf16[2,3,180,256]{3,2,1,0:T(8,128)(2,1)S(1)}) fusion(f32[2,3,180,256]{3,2,1,0:T(8,128)} %get-tuple-element.70, f32[2,3,180]{2,1,0:T(4,128)S(1)} %get-tuple-element.56, f32[2,3,180]{2,1,0:T(4,128)S(1)} %get-tuple-element.55, f32[2,3,180]{2,1,0:T(4,128)S(1)} %fusion.115, ...), kind=kLoop, calls=%fused_computation.95 | loop fusion | flops 6082560 | bytes 5011200 | tf_op jit(solution)/shard_map/convert_element_type | solution.py:309
  215.5 1.2 copy.131
  216.7 1.2 copy.130
  (111 shorter events, 9.8 us)
Async XLA Ops:
  7.2 105.8 %copy-start = (bf16[1024,1024]{1,0:T(8,128)(2,1)S(1)}, bf16[1024,1024]{1,0:T(8,128)(2,1)}, u32[]{:S(2)}) copy-start(bf16[1024,1024]{1,0:T(8,128)(2,1)} %param.14) | copy-start | bytes 6291460
  7.2 9.0 %copy-start.13 = (f32[2,2,128,128]{3,2,1,0:T(8,128)S(1)}, f32[2,2,128,128]{3,2,1,0:T(8,128)}, u32[]{:S(2)}) copy-start(f32[2,2,128,128]{3,2,1,0:T(8,128)} %param.10) | copy-start | bytes 786436
  7.2 50.5 %all-gather.3.cloned.1.call-start = ((), (), s32[]{:S(2)}) async-start(), calls=%async_computation.6 | async-start | bytes 2764800 | tf_op jit(solution)/shard_map/all_gather | solution.py:229
  9.0 7.3 %copy-start.14 = (f32[2,2,128,128]{3,2,1,0:T(8,128)S(1)}, f32[2,2,128,128]{3,2,1,0:T(8,128)}, u32[]{:S(2)}) copy-start(f32[2,2,128,128]{3,2,1,0:T(8,128)} %param.12) | copy-start | bytes 786436
  9.0 10.5 %collective-permute-start.1 = (f32[2,2,3,180]{3,2,1,0:T(4,128)S(1)}, f32[2,2,3,180]{3,2,1,0:T(4,128)S(1)}, u32[]{:S(2)}, u32[]{:S(2)}) collective-permute-start(f32[2,2,3,180]{3,2,1,0:T(4,128)S(1)} %get-tuple-element.64), channel_id=1, source_target_pairs={{0,2},{1,3},{2,0},{3,1},{4,6},{5,7},{6,4},{7,5},{8,10},{9,11},{10,... | collective-permute-start | bytes 25928 | tf_op jit(solution)/shard_map/ppermute | solution.py:164
  12.3 7.2 %collective-permute-start = (f32[2,2,3,180]{3,2,1,0:T(4,128)S(1)}, f32[2,2,3,180]{3,2,1,0:T(4,128)S(1)}, u32[]{:S(2)}, u32[]{:S(2)}) collective-permute-start(f32[2,2,3,180]{3,2,1,0:T(4,128)S(1)} %get-tuple-element.64), channel_id=1, source_target_pairs={{0,3},{1,0},{2,1},{3,2},{4,7},{5,4},{6,5},{7,6},{8,11},{9,8},{10,9... | collective-permute-start | bytes 25928 | tf_op jit(solution)/shard_map/ppermute | solution.py:164
  13.4 6.1 %collective-permute-start.2 = (f32[2,2,3,180]{3,2,1,0:T(4,128)S(1)}, f32[2,2,3,180]{3,2,1,0:T(4,128)S(1)}, u32[]{:S(2)}, u32[]{:S(2)}) collective-permute-start(f32[2,2,3,180]{3,2,1,0:T(4,128)S(1)} %get-tuple-element.64), channel_id=1, source_target_pairs={{0,1},{1,2},{2,3},{3,0},{4,5},{5,6},{6,7},{7,4},{8,9},{9,10},{10,1... | collective-permute-start | bytes 25928 | tf_op jit(solution)/shard_map/ppermute | solution.py:164
  14.4 96.0 %all-gather.5.cloned.1.call-start = ((), (), s32[]{:S(2)}) async-start(), calls=%async_computation.7 | async-start | bytes 2826240 | tf_op jit(solution)/shard_map/all_gather | solution.py:252
  18.4 1.8 copy-start.2
  19.5 3.6 %copy-start.20 = (s32[1024]{0:T(1024)}, s32[1024]{0:T(1024)S(1)}, u32[]{:S(2)}) copy-start(s32[1024]{0:T(1024)S(1)} %pad_clamp_fusion) | copy-start | bytes 12292
  51.2 1.6 copy-start.21
  52.9 2.1 copy-start.6
  52.9 2.1 copy-start.22
  55.7 1.0 copy-start.1
  59.7 15.8 %copy-start.3 = (bf16[2,3,180,256]{3,0,2,1:T(2,128)(2,1)S(1)}, bf16[2,3,180,256]{3,0,2,1:T(2,128)(2,1)}, u32[]{:S(2)}) copy-start(bf16[2,3,180,256]{3,0,2,1:T(2,128)(2,1)} %param.8) | copy-start | bytes 1658884
  59.7 15.8 %copy-start.15 = (bf16[2,180,96]{2,1,0:T(8,128)(2,1)S(1)}, bf16[2,180,96]{2,1,0:T(8,128)(2,1)}, u32[]{:S(2)}) copy-start(bf16[2,180,96]{2,1,0:T(8,128)(2,1)} %pad_maximum_fusion.3) | copy-start | bytes 207364
  76.9 76.8 %reduce-scatter.5.cloned.1.call-start = ((), (), s32[]{:S(2)}) async-start(), calls=%async_computation.9 | async-start | bytes 2826240 | tf_op jit(solution)/shard_map/reduce_scatter | solution.py:196
  110.4 2.6 %copy-start.8 = (bf16[2,3,180,1024]{3,2,1,0:T(8,128)(2,1)S(1)}, bf16[2,3,180,1024]{3,2,1,0:T(8,128)(2,1)}, u32[]{:S(2)}) copy-start(bf16[2,3,180,1024]{3,2,1,0:T(8,128)(2,1)} %all-gather.5.cloned.1.call-done) | copy-start | bytes 6635524
  110.4 5.5 %slice-start = ((s8[4521984]{0:T(1024)(128)(4,1)}), s8[4194304]{0:T(1024)(128)(4,1)S(1)}, s32[]{:S(2)}) async-start(s8[4521984]{0:T(1024)(128)(4,1)} %bitcast.320), calls=%async_computation.10 | async-start | bytes 8388608
  113.0 2.9 %copy-start.16 = (f32[2,3,180]{2,1,0:T(4,128)}, f32[2,3,180]{2,1,0:T(4,128)S(1)}, u32[]{:S(2)}) copy-start(f32[2,3,180]{2,1,0:T(4,128)S(1)} %get-tuple-element.65) | copy-start | bytes 12964
  113.0 2.9 %copy-start.18 = (f32[2,3,180]{2,1,0:T(4,128)}, f32[2,3,180]{2,1,0:T(4,128)S(1)}, u32[]{:S(2)}) copy-start(f32[2,3,180]{2,1,0:T(4,128)S(1)} %get-tuple-element.66) | copy-start | bytes 12964
  113.0 2.9 %slice-start.1 = ((s8[4521984]{0:T(1024)(128)(4,1)}), s8[327680]{0:T(1024)(128)(4,1)S(1)}, s32[]{:S(2)}) async-start(s8[4521984]{0:T(1024)(128)(4,1)} %bitcast.320), calls=%async_computation.11 | async-start | bytes 655360
  115.9 5.4 %copy-start.23 = (f32[2,3,180,1024]{3,2,1,0:T(8,128)}, f32[2,3,180,1024]{3,2,1,0:T(8,128)S(1)}, u32[]{:S(2)}) copy-start(f32[2,3,180,1024]{3,2,1,0:T(8,128)S(1)} %fusion.14) | copy-start | bytes 13271044
  121.4 90.7 %reduce-scatter.3.cloned.1.call-start = ((), (), s32[]{:S(2)}) async-start(), calls=%async_computation.8 | async-start | bytes 2826240 | tf_op jit(solution)/shard_map/reduce_scatter | solution.py:196
  128.4 5.3 %collective-permute-start.4 = (f32[2,2,3,180]{3,2,1,0:T(4,128)S(1)}, f32[2,2,3,180]{3,2,1,0:T(4,128)S(1)}, u32[]{:S(2)}, u32[]{:S(2)}) collective-permute-start(f32[2,2,3,180]{3,2,1,0:T(4,128)S(1)} %get-tuple-element.62), channel_id=1, source_target_pairs={{0,2},{1,3},{2,0},{3,1},{4,6},{5,7},{6,4},{7,5},{8,10},{9,11},{10,... | collective-permute-start | bytes 25928 | tf_op jit(solution)/shard_map/ppermute | solution.py:164
  131.1 4.0 %collective-permute-start.3 = (f32[2,2,3,180]{3,2,1,0:T(4,128)S(1)}, f32[2,2,3,180]{3,2,1,0:T(4,128)S(1)}, u32[]{:S(2)}, u32[]{:S(2)}) collective-permute-start(f32[2,2,3,180]{3,2,1,0:T(4,128)S(1)} %get-tuple-element.62), channel_id=1, source_target_pairs={{0,3},{1,0},{2,1},{3,2},{4,7},{5,4},{6,5},{7,6},{8,11},{9,8},{10,9... | collective-permute-start | bytes 25928 | tf_op jit(solution)/shard_map/ppermute | solution.py:164
  131.9 5.3 %collective-permute-start.5 = (f32[2,2,3,180]{3,2,1,0:T(4,128)S(1)}, f32[2,2,3,180]{3,2,1,0:T(4,128)S(1)}, u32[]{:S(2)}, u32[]{:S(2)}) collective-permute-start(f32[2,2,3,180]{3,2,1,0:T(4,128)S(1)} %get-tuple-element.62), channel_id=1, source_target_pairs={{0,1},{1,2},{2,3},{3,0},{4,5},{5,6},{6,7},{7,4},{8,9},{9,10},{10,1... | collective-permute-start | bytes 25928 | tf_op jit(solution)/shard_map/ppermute | solution.py:164
  179.7 2.1 copy-start.5
  182.1 1.0 copy-start.10
  183.5 17.1 %copy-start.12 = (bf16[2,3,180,256]{3,2,1,0:T(8,128)(2,1)S(1)}, bf16[2,3,180,256]{3,2,1,0:T(8,128)(2,1)}, u32[]{:S(2)}) copy-start(bf16[2,3,180,256]{3,2,1,0:T(8,128)(2,1)} %reduce-scatter.5.cloned.1.call-done) | copy-start | bytes 1658884
  184.1 16.5 %copy-start.4 = (bf16[2,3,180,256]{3,0,2,1:T(2,128)(2,1)S(1)}, bf16[2,3,180,256]{3,0,2,1:T(2,128)(2,1)}, u32[]{:S(2)}) copy-start(bf16[2,3,180,256]{3,0,2,1:T(2,128)(2,1)} %param.8) | copy-start | bytes 1658884
  184.2 16.5 %copy-start.7 = (bf16[2,3,180,256]{3,2,1,0:T(8,128)(2,1)S(1)}, bf16[2,3,180,256]{3,2,1,0:T(8,128)(2,1)}, u32[]{:S(2)}) copy-start(bf16[2,3,180,256]{3,2,1,0:T(8,128)(2,1)} %fusion.37) | copy-start | bytes 1658884
  184.2 16.5 %copy-start.9 = (bf16[2,3,180,256]{3,0,2,1:T(2,128)(2,1)S(1)}, bf16[2,3,180,256]{3,0,2,1:T(2,128)(2,1)}, u32[]{:S(2)}) copy-start(bf16[2,3,180,256]{3,0,2,1:T(2,128)(2,1)} %param.9) | copy-start | bytes 1658884
  184.2 16.5 %copy-start.11 = (f32[2,180,96]{2,1,0:T(8,128)S(1)}, f32[2,180,96]{2,1,0:T(8,128)}, u32[]{:S(2)}) copy-start(f32[2,180,96]{2,1,0:T(8,128)} %pad_maximum_fusion.2) | copy-start | bytes 414724
  184.2 16.5 %copy-start.17 = (f32[2,3,180]{2,1,0:T(4,128)S(1)}, f32[2,3,180]{2,1,0:T(4,128)}, u32[]{:S(2)}) copy-start(f32[2,3,180]{2,1,0:T(4,128)} %copy-done.16) | copy-start | bytes 12964
  184.2 16.5 %copy-start.19 = (f32[2,3,180]{2,1,0:T(4,128)S(1)}, f32[2,3,180]{2,1,0:T(4,128)}, u32[]{:S(2)}) copy-start(f32[2,3,180]{2,1,0:T(4,128)} %copy-done.18) | copy-start | bytes 12964
  203.4 5.3 %collective-permute-start.7 = (f32[2,2,3,180]{3,2,1,0:T(4,128)S(1)}, f32[2,2,3,180]{3,2,1,0:T(4,128)S(1)}, u32[]{:S(2)}, u32[]{:S(2)}) collective-permute-start(f32[2,2,3,180]{3,2,1,0:T(4,128)S(1)} %get-tuple-element.58), channel_id=1, source_target_pairs={{0,2},{1,3},{2,0},{3,1},{4,6},{5,7},{6,4},{7,5},{8,10},{9,11},{10,... | collective-permute-start | bytes 25928 | tf_op jit(solution)/shard_map/ppermute | solution.py:164
  204.7 4.0 %collective-permute-start.6 = (f32[2,2,3,180]{3,2,1,0:T(4,128)S(1)}, f32[2,2,3,180]{3,2,1,0:T(4,128)S(1)}, u32[]{:S(2)}, u32[]{:S(2)}) collective-permute-start(f32[2,2,3,180]{3,2,1,0:T(4,128)S(1)} %get-tuple-element.58), channel_id=1, source_target_pairs={{0,3},{1,0},{2,1},{3,2},{4,7},{5,4},{6,5},{7,6},{8,11},{9,8},{10,9... | collective-permute-start | bytes 25928 | tf_op jit(solution)/shard_map/ppermute | solution.py:164
  206.3 4.9 %collective-permute-start.8 = (f32[2,2,3,180]{3,2,1,0:T(4,128)S(1)}, f32[2,2,3,180]{3,2,1,0:T(4,128)S(1)}, u32[]{:S(2)}, u32[]{:S(2)}) collective-permute-start(f32[2,2,3,180]{3,2,1,0:T(4,128)S(1)} %get-tuple-element.58), channel_id=1, source_target_pairs={{0,1},{1,2},{2,3},{3,0},{4,5},{5,6},{6,7},{7,4},{8,9},{9,10},{10,1... | collective-permute-start | bytes 25928 | tf_op jit(solution)/shard_map/ppermute | solution.py:164
Sparse Core Ops, SparseCore 0:
  14.5 36.8 all-gather.2
  77.1 33.2 all-gather.4
  121.5 32.2 reduce-scatter.4
  156.2 30.4 reduce-scatter.2

commit v3 on v2

--- a/solution.py
+++ b/solution.py
@@ -157,7 +157,6 @@
 def token_sums(first_term, second_term):
     pair = jnp.stack([first_term, second_term])
     count = lax.axis_size("feat")
-    position = lax.axis_index("feat")
     shifted = jnp.stack(
         [pair]
         + [
@@ -165,10 +164,9 @@
             for shift in range(1, count)
         ]
     )
-    ordered = shifted[(jnp.arange(count) + count - position) % count]
-    total = ordered[0]
+    total = shifted[0]
     for source in range(1, count):
-        total = total + ordered[source]
+        total = total + shifted[source]
     return (total[0], total[1])
 
 

time: 225 us -> 220 us (0.978)
  starting transfers between devices: 13.7 us -> 17.6 us
  waiting for transfers between devices: 49.5 us -> 45.9 us
  local copies, waits for them, and re-layouts: 16 us -> 13.2 us
    ppermute x9, waiting for transfers between devices: 8.56 us -> 3.66 us  [token_sums(): lax.ppermute(pair, 'feat', [(i, (i + count - shift) % count) for i in ran...]
    ppermute x9, starting transfers between devices: 13.5 us -> 17.4 us  [token_sums(): lax.ppermute(pair, 'feat', [(i, (i + count - shift) % count) for i in ran...]
    reduce_scatter x2, waiting for transfers between devices: 14.4 us -> 17.4 us  [channel_share(): lax.psum_scatter(term.astype(jnp.bfloat16), 'feat', scatter_dimension=3,...]
    gather x3 -> x0, local copies, waits for them, and re-layouts: 2.85 us -> none  [token_sums(): ordered = shifted[(jnp.arange(count) + count - position) % count]]
  transfers between devices with their start and end apart: 13 -> 13, of which waited for: 7 -> 5; matrix products, arithmetic and copies ran while one was open for 21% -> 19% of each run, Pallas kernels for 0% -> 0%
where the time goes in v3:
time: 220 us; the launch traced here: 219 us
  blocking collectives  77.2 us (35%)
  waiting for transfers between devices  45.9 us (21%)
  matrix products  38.3 us (17%)
  starting transfers between devices  17.6 us (8%)
  between operations  14.4 us (7%)
  local copies, waits for them, and re-layouts  13.2 us (6%)
  other arithmetic  12.9 us (6%)
    all_to_all x2, blocking collectives, stacked_columns(): lax.all_to_all(field.astype(link_type), 'space', 3, 2, tiled=True)  45.9 us
    all_to_all x2, blocking collectives, stacked_rows(): lax.all_to_all(field.astype(link_type), 'space', 2, 3, tiled=True)  31.3 us
    all_gather x1, waiting for transfers between devices, per_device(): whole_residual = lax.all_gather(residual, 'feat', axis=3, tiled=True)  24.8 us
    ppermute x9, starting transfers between devices, token_sums(): lax.ppermute(pair, 'feat', [(i, (i + count - shift) % count) for i in ran...  17.4 us
    reduce_scatter x2, waiting for transfers between devices, channel_share(): lax.psum_scatter(term.astype(jnp.bfloat16), 'feat', scatter_dimension=3,...  17.4 us
    dot_general x1, matrix products, per_device(): jnp.einsum('brwd,hd->brwh', whole_cotangent, down_weight, preferred_eleme...  6.92 us
    dot_general x1, matrix products, per_device(): jnp.einsum('brwh,hd->brwd', activated, down_weight, preferred_element_typ...  6.91 us
    dot_general x1, matrix products, per_device(): jnp.einsum('brwh,dh->brwd', grad_hidden, up_weight, preferred_element_typ...  5.41 us
  transfers between devices with their start and end apart: 13, of which 5 were waited for; matrix products, arithmetic and copies ran while one was open for 19% of the time, Pallas kernels for 0%

profile of v3, /device:TPU:0, one launch (start us, length us, event | category | flops | bytes accessed | tf_op | source)
XLA Modules:
  0.0 219.4 jit_solution(13806531281613694137)
XLA Ops:
  7.2 1.7 convert_reduce_fusion.1
  9.0 3.4 %collective-permute-start.1 = (f32[2,2,3,180]{3,2,1,0:T(4,128)S(1)}, f32[2,2,3,180]{3,2,1,0:T(4,128)S(1)}, u32[]{:S(2)}, u32[]{:S(2)}) collective-permute-start(f32[2,2,3,180]{3,2,1,0:T(4,128)S(1)} %pad_maximum_fusion.8), channel_id=1, source_target_pairs={{0,2},{1,3},{2,0},{3,1},{4,6},{5,7},{6,4},{7,5},{8,10},{9,11},{10,... | collective-permute-start | bytes 25928 | tf_op jit(solution)/shard_map/ppermute | solution.py:163
  12.3 0.7 collective-permute-start.2
  13.0 2.6 %collective-permute-start = (f32[2,2,3,180]{3,2,1,0:T(4,128)S(1)}, f32[2,2,3,180]{3,2,1,0:T(4,128)S(1)}, u32[]{:S(2)}, u32[]{:S(2)}) collective-permute-start(f32[2,2,3,180]{3,2,1,0:T(4,128)S(1)} %pad_maximum_fusion.8), channel_id=1, source_target_pairs={{0,3},{1,0},{2,1},{3,2},{4,7},{5,4},{6,5},{7,6},{8,11},{9,8},{10,9... | collective-permute-start | bytes 25928 | tf_op jit(solution)/shard_map/ppermute | solution.py:163
  17.5 0.7 pad_maximum_fusion.1
  18.3 1.1 maximum_bitcast_fusion.1
  19.4 0.7 pad_maximum_fusion.3
  20.2 1.0 convolution_bitcast_fusion.7
  21.2 0.9 copy.96
  22.1 27.1 %all_to_all.72 = f32[2,2,3,96,256]{4,1,2,0,3:T(2,128)S(1)} all-to-all(f32[2,2,3,96,256]{4,1,2,0,3:T(2,128)S(1)} %copy.96), channel_id=1, replica_groups=mesh['space'=32,'feat'=4] {'space'}, dimensions={3} | all-to-all | bytes 2359296 | tf_op jit(solution)/shard_map/all_to_all | solution.py:150
  49.6 0.7 convolution_bitcast_fusion.6
  50.3 1.6 reshape.195
  51.9 2.1 fusion.31
  54.0 0.7 fusion.32
  54.7 1.0 copy-done.1
  55.7 1.0 copy_bitcast_fusion
  56.7 1.4 fusion.42
  58.1 0.6 copy.108
  58.8 15.3 %all_to_all.73 = bf16[2,2,96,3,256]{4,0,3,1,2:T(2,128)(2,1)S(1)} all-to-all(bf16[2,2,96,3,256]{4,0,3,1,2:T(2,128)(2,1)S(1)} %copy.108), channel_id=1, replica_groups=mesh['space'=32,'feat'=4] {'space'}, dimensions={2} | all-to-all | bytes 1179648 | tf_op jit(solution)/shard_map/all_to_all | solution.py:154
  74.1 0.5 copy.110
  74.6 1.3 fusion.37
  76.0 6.9 %fusion.16 = f32[2,3,180,1024]{3,2,1,0:T(8,128)} fusion(bf16[2,3,180,1024]{3,0,2,1:T(2,128)(2,1)} %all-gather.3.cloned.1.call-done, bf16[1024,1024]{1,0:T(8,128)(2,1)} %param.15), kind=kOutput, calls=%fused_computation.20 | convolution fusion | flops 2264924160 | bytes 8732672 | tf_op jit(solution)/shard_map/brwd,hd->brwh/dot_general | solution.py:251
  82.9 24.8 %all-gather.5.cloned.1.call-done = bf16[2,3,180,1024]{3,2,1,0:T(8,128)(2,1)} async-done(((bf16[2,3,180,256]{3,2,1,0:T(8,128)(2,1)}), bf16[2,3,180,1024]{3,2,1,0:T(8,128)(2,1)}) %all-gather.5.cloned.1.call-update) | async-done | bytes 2211856 | tf_op jit(solution)/shard_map/all_gather | solution.py:250
  107.7 2.5 %convert_reduce_fusion = (f32[2,3,180]{2,1,0:T(4,128)S(1)}, f32[2,3,180]{2,1,0:T(4,128)S(1)}) fusion(bf16[2,3,180,1024]{3,2,1,0:T(8,128)(2,1)} %all-gather.5.cloned.1.call-done), kind=kLoop, calls=%fused_computation.3 | loop fusion | flops 4421520 | bytes 2220480 | tf_op jit(solution)/shard_map/reduce_sum | solution.py:256
  110.3 2.8 %fusion.14 = f32[2,3,180,1024]{3,2,1,0:T(8,128)S(1)} fusion(bf16[2,3,180,1024]{3,2,1,0:T(8,128)(2,1)S(1)} %copy-done.8, f32[2,3,180]{2,1,0:T(4,128)S(1)} %get-tuple-element.60, f32[2,3,180]{2,1,0:T(4,128)S(1)} %get-tuple-element.59, bf16[1024,1024]{1,0:T(8,128)(2,1)S(1)} %copy-done), kind=kOutput, calls=%fused_computation.19 | convolution fusion | flops 2269347840 | bytes 8741312 | tf_op jit(solution)/shard_map/brwd,dh->brwh/dot_general | solution.py:260
  113.2 5.4 %fusion.123 = (f32[2,3,180]{2,1,0:T(4,128)S(1)}, f32[2,3,180]{2,1,0:T(4,128)S(1)}, bf16[2,3,180,1024]{3,2,1,0:T(8,128)(2,1)}) fusion(f32[2,3,180]{2,1,0:T(4,128)S(1)} %get-tuple-element.60, f32[2,3,180]{2,1,0:T(4,128)S(1)} %get-tuple-element.59, bf16[2,3,180,1024]{3,2,1,0:T(8,128)(2,1)S(1)} %copy-done.8, bf16[1024,1024]{1,0:T(8,128)(2,1)S(1)} %copy-done, ...), kind=kOutput, calls=%fused_computation.189 | convolution fusion | flops 2283722752 | bytes 15385472 | tf_op jit(solution)/shard_map/brwh,dh->brwd/dot_general | solution.py:269
  118.7 6.9 %fusion.28 = bf16[2,3,180,1024]{3,2,1,0:T(8,128)(2,1)} fusion(bf16[1024,1024]{1,0:T(8,128)(2,1)} %param.15, f32[2,3,180,1024]{3,2,1,0:T(8,128)} %copy-done.19), kind=kOutput, calls=%fused_computation.36 | convolution fusion | flops 2271559680 | bytes 8732672 | tf_op jit(solution)/shard_map/brwh,hd->brwd/dot_general | solution.py:264
  125.6 2.8 %collective-permute-start.4 = (f32[2,2,3,180]{3,2,1,0:T(4,128)S(1)}, f32[2,2,3,180]{3,2,1,0:T(4,128)S(1)}, u32[]{:S(2)}, u32[]{:S(2)}) collective-permute-start(f32[2,2,3,180]{3,2,1,0:T(4,128)S(1)} %pad_maximum_fusion.9), channel_id=1, source_target_pairs={{0,2},{1,3},{2,0},{3,1},{4,6},{5,7},{6,4},{7,5},{8,10},{9,11},{10,... | collective-permute-start | bytes 25928 | tf_op jit(solution)/shard_map/ppermute | solution.py:163
  128.6 3.0 %collective-permute-start.3 = (f32[2,2,3,180]{3,2,1,0:T(4,128)S(1)}, f32[2,2,3,180]{3,2,1,0:T(4,128)S(1)}, u32[]{:S(2)}, u32[]{:S(2)}) collective-permute-start(f32[2,2,3,180]{3,2,1,0:T(4,128)S(1)} %pad_maximum_fusion.9), channel_id=1, source_target_pairs={{0,3},{1,0},{2,1},{3,2},{4,7},{5,4},{6,5},{7,6},{8,11},{9,8},{10,9... | collective-permute-start | bytes 25928 | tf_op jit(solution)/shard_map/ppermute | solution.py:163
  131.7 1.9 collective-permute-done.5
  133.6 17.3 %reduce-scatter.5.cloned.1.call-done = bf16[2,3,180,256]{3,2,1,0:T(8,128)(2,1)} async-done(((bf16[2,3,180,1024]{3,2,1,0:T(8,128)(2,1)}), bf16[2,3,180,256]{3,2,1,0:T(8,128)(2,1)}) %reduce-scatter.5.cloned.1.call-update) | async-done | bytes 552976 | tf_op jit(solution)/shard_map/reduce_scatter | solution.py:194
  151.0 2.3 %fusion.40 = bf16[2,2,3,96,256]{4,3,2,1,0:T(8,128)(2,1)S(1)} fusion(bf16[2,180,96]{2,1,0:T(8,128)(2,1)} %pad_maximum_fusion.3, bf16[2,3,180,256]{3,2,1,0:T(8,128)(2,1)} %fusion.37, bf16[2,3,180,256]{3,2,1,0:T(8,128)(2,1)} %reduce-scatter.5.cloned.1.call-done, bf16[2,3,180,256]{3,0,2,1:T(2,128)(2,1)} %param.9, f32[2,3,180]{2,1,0:T(4,128)S(1)} %get-tuple-element.58, ...), kind=kOutput, calls=%fused_computation.61 | convolution fusion | flops 108933120 | bytes 2335104 | tf_op jit(solution)/shard_map/brwc,pwk->pbrkc/dot_general | solution.py:130
  153.3 0.6 copy.114
  153.9 18.8 %all_to_all.74 = bf16[2,2,3,96,256]{4,1,2,0,3:T(2,128)(2,1)S(1)} all-to-all(bf16[2,2,3,96,256]{4,1,2,0,3:T(2,128)(2,1)S(1)} %copy.114), channel_id=1, replica_groups=mesh['space'=32,'feat'=4] {'space'}, dimensions={3} | all-to-all | bytes 1179648 | tf_op jit(solution)/shard_map/all_to_all | solution.py:150
  173.2 1.2 convolution_bitcast_fusion.8
  174.4 2.5 %reshape.229 = bf16[2,2,96,3,2,128]{5,4,2,0,3,1:T(2,128)(2,1)} reshape(bf16[2,2,96,3,256]{4,2,0,3,1:T(8,128)(2,1)} %convolution_bitcast_fusion.8) | data formatting | bytes 1179648 | tf_op jit(solution)/shard_map/reshape | solution.py:61
  176.9 2.1 fusion.39
  179.3 0.6 copy.189
  180.7 0.6 copy.126
  181.3 15.9 %all_to_all.75 = bf16[2,2,96,3,256]{4,0,3,1,2:T(2,128)(2,1)S(1)} all-to-all(bf16[2,2,96,3,256]{4,0,3,1,2:T(2,128)(2,1)S(1)} %copy.126), channel_id=1, replica_groups=mesh['space'=32,'feat'=4] {'space'}, dimensions={2} | all-to-all | bytes 1179648 | tf_op jit(solution)/shard_map/all_to_all | solution.py:154
  197.8 2.7 %fusion.124 = (f32[2,3,180]{2,1,0:T(4,128)S(1)}, f32[2,3,180]{2,1,0:T(4,128)S(1)}, f32[2,3,180,256]{3,2,1,0:T(8,128)}) fusion(f32[2,3,180]{2,1,0:T(4,128)S(1)} %fusion.115, f32[2,3,180]{2,1,0:T(4,128)S(1)} %fusion.116, bf16[2,3,180,256]{3,0,2,1:T(2,128)(2,1)S(1)} %copy-done.4, bf16[2,2,3,96,256]{4,1,3,2,0:T(2,128)(2,1)S(1)} %bitcast.284, ...), kind=kOutput, calls=%fused_computation.190 | convolution fusion | flops 110866320 | bytes 4080384 | tf_op jit(solution)/shard_map/pbrkc,pwk->brwc/dot_general | solution.py:134
  200.5 1.5 collective-permute-start.7
  202.4 2.9 %collective-permute-start.6 = (f32[2,2,3,180]{3,2,1,0:T(4,128)S(1)}, f32[2,2,3,180]{3,2,1,0:T(4,128)S(1)}, u32[]{:S(2)}, u32[]{:S(2)}) collective-permute-start(f32[2,2,3,180]{3,2,1,0:T(4,128)S(1)} %pad_maximum_fusion.10), channel_id=1, source_target_pairs={{0,3},{1,0},{2,1},{3,2},{4,7},{5,4},{6,5},{7,6},{8,11},{9,8},{10,9... | collective-permute-start | bytes 25928 | tf_op jit(solution)/shard_map/ppermute | solution.py:163
  205.3 0.5 collective-permute-done.7
  205.8 1.2 collective-permute-done.8
  207.0 3.4 %fusion.68 = (bf16[2,3,180,256]{3,2,1,0:T(8,128)(2,1)S(1)}, bf16[2,3,180,256]{3,2,1,0:T(8,128)(2,1)S(1)}) fusion(f32[2,3,180,256]{3,2,1,0:T(8,128)} %get-tuple-element.64, f32[2,3,180]{2,1,0:T(4,128)S(1)} %get-tuple-element.56, f32[2,3,180]{2,1,0:T(4,128)S(1)} %get-tuple-element.55, f32[2,3,180]{2,1,0:T(4,128)S(1)} %fusion.115, ...), kind=kLoop, calls=%fused_computation.92 | loop fusion | flops 6082560 | bytes 5011200 | tf_op jit(solution)/shard_map/convert_element_type | solution.py:307
  210.4 1.2 copy.131
  211.6 1.2 copy.130
  (95 shorter events, 5.2 us)
Async XLA Ops:
  7.2 103.1 %copy-start = (bf16[1024,1024]{1,0:T(8,128)(2,1)S(1)}, bf16[1024,1024]{1,0:T(8,128)(2,1)}, u32[]{:S(2)}) copy-start(bf16[1024,1024]{1,0:T(8,128)(2,1)} %param.14) | copy-start | bytes 6291460
  7.2 10.2 %copy-start.14 = (f32[2,2,128,128]{3,2,1,0:T(8,128)S(1)}, f32[2,2,128,128]{3,2,1,0:T(8,128)}, u32[]{:S(2)}) copy-start(f32[2,2,128,128]{3,2,1,0:T(8,128)} %param.10) | copy-start | bytes 786436
  7.2 49.5 %all-gather.3.cloned.1.call-start = ((), (), s32[]{:S(2)}) async-start(), calls=%async_computation.6 | async-start | bytes 2764800 | tf_op jit(solution)/shard_map/all_gather | solution.py:227
  9.0 8.5 %copy-start.15 = (f32[2,2,128,128]{3,2,1,0:T(8,128)S(1)}, f32[2,2,128,128]{3,2,1,0:T(8,128)}, u32[]{:S(2)}) copy-start(f32[2,2,128,128]{3,2,1,0:T(8,128)} %param.12) | copy-start | bytes 786436
  9.0 11.1 %collective-permute-start.1 = (f32[2,2,3,180]{3,2,1,0:T(4,128)S(1)}, f32[2,2,3,180]{3,2,1,0:T(4,128)S(1)}, u32[]{:S(2)}, u32[]{:S(2)}) collective-permute-start(f32[2,2,3,180]{3,2,1,0:T(4,128)S(1)} %pad_maximum_fusion.8), channel_id=1, source_target_pairs={{0,2},{1,3},{2,0},{3,1},{4,6},{5,7},{6,4},{7,5},{8,10},{9,11},{10,... | collective-permute-start | bytes 25928 | tf_op jit(solution)/shard_map/ppermute | solution.py:163
  12.3 7.8 %collective-permute-start.2 = (f32[2,2,3,180]{3,2,1,0:T(4,128)S(1)}, f32[2,2,3,180]{3,2,1,0:T(4,128)S(1)}, u32[]{:S(2)}, u32[]{:S(2)}) collective-permute-start(f32[2,2,3,180]{3,2,1,0:T(4,128)S(1)} %pad_maximum_fusion.8), channel_id=1, source_target_pairs={{0,1},{1,2},{2,3},{3,0},{4,5},{5,6},{6,7},{7,4},{8,9},{9,10},{10,1... | collective-permute-start | bytes 25928 | tf_op jit(solution)/shard_map/ppermute | solution.py:163
  13.0 7.1 %collective-permute-start = (f32[2,2,3,180]{3,2,1,0:T(4,128)S(1)}, f32[2,2,3,180]{3,2,1,0:T(4,128)S(1)}, u32[]{:S(2)}, u32[]{:S(2)}) collective-permute-start(f32[2,2,3,180]{3,2,1,0:T(4,128)S(1)} %pad_maximum_fusion.8), channel_id=1, source_target_pairs={{0,3},{1,0},{2,1},{3,2},{4,7},{5,4},{6,5},{7,6},{8,11},{9,8},{10,9... | collective-permute-start | bytes 25928 | tf_op jit(solution)/shard_map/ppermute | solution.py:163
  15.6 92.1 %all-gather.5.cloned.1.call-start = ((), (), s32[]{:S(2)}) async-start(), calls=%async_computation.7 | async-start | bytes 2826240 | tf_op jit(solution)/shard_map/all_gather | solution.py:250
  17.5 2.6 %copy-start.11 = (f32[2,180,96]{2,1,0:T(8,128)}, f32[2,180,96]{2,1,0:T(8,128)S(1)}, u32[]{:S(2)}) copy-start(f32[2,180,96]{2,1,0:T(8,128)S(1)} %pad_maximum_fusion.2) | copy-start | bytes 414724
  18.3 1.8 copy-start.2
  50.3 1.6 copy-start.17
  51.9 2.1 copy-start.6
  51.9 2.1 copy-start.18
  54.7 1.0 copy-start.1
  58.7 15.8 %copy-start.3 = (bf16[2,3,180,256]{3,0,2,1:T(2,128)(2,1)S(1)}, bf16[2,3,180,256]{3,0,2,1:T(2,128)(2,1)}, u32[]{:S(2)}) copy-start(bf16[2,3,180,256]{3,0,2,1:T(2,128)(2,1)} %param.8) | copy-start | bytes 1658884
  58.7 15.8 %copy-start.16 = (bf16[2,180,96]{2,1,0:T(8,128)(2,1)S(1)}, bf16[2,180,96]{2,1,0:T(8,128)(2,1)}, u32[]{:S(2)}) copy-start(bf16[2,180,96]{2,1,0:T(8,128)(2,1)} %pad_maximum_fusion.3) | copy-start | bytes 207364
  75.9 75.0 %reduce-scatter.5.cloned.1.call-start = ((), (), s32[]{:S(2)}) async-start(), calls=%async_computation.9 | async-start | bytes 2826240 | tf_op jit(solution)/shard_map/reduce_scatter | solution.py:194
  107.7 2.6 %copy-start.8 = (bf16[2,3,180,1024]{3,2,1,0:T(8,128)(2,1)S(1)}, bf16[2,3,180,1024]{3,2,1,0:T(8,128)(2,1)}, u32[]{:S(2)}) copy-start(bf16[2,3,180,1024]{3,2,1,0:T(8,128)(2,1)} %all-gather.5.cloned.1.call-done) | copy-start | bytes 6635524
  107.7 5.4 %slice-start = ((s8[4521984]{0:T(1024)(128)(4,1)}), s8[4194304]{0:T(1024)(128)(4,1)S(1)}, s32[]{:S(2)}) async-start(s8[4521984]{0:T(1024)(128)(4,1)} %bitcast.300), calls=%async_computation.10 | async-start | bytes 8388608
  110.3 2.9 %slice-start.1 = ((s8[4521984]{0:T(1024)(128)(4,1)}), s8[327680]{0:T(1024)(128)(4,1)S(1)}, s32[]{:S(2)}) async-start(s8[4521984]{0:T(1024)(128)(4,1)} %bitcast.300), calls=%async_computation.11 | async-start | bytes 655360
  113.2 5.4 %copy-start.19 = (f32[2,3,180,1024]{3,2,1,0:T(8,128)}, f32[2,3,180,1024]{3,2,1,0:T(8,128)S(1)}, u32[]{:S(2)}) copy-start(f32[2,3,180,1024]{3,2,1,0:T(8,128)S(1)} %fusion.14) | copy-start | bytes 13271044
  118.6 88.4 %reduce-scatter.3.cloned.1.call-start = ((), (), s32[]{:S(2)}) async-start(), calls=%async_computation.8 | async-start | bytes 2826240 | tf_op jit(solution)/shard_map/reduce_scatter | solution.py:194
  125.6 6.0 %collective-permute-start.4 = (f32[2,2,3,180]{3,2,1,0:T(4,128)S(1)}, f32[2,2,3,180]{3,2,1,0:T(4,128)S(1)}, u32[]{:S(2)}, u32[]{:S(2)}) collective-permute-start(f32[2,2,3,180]{3,2,1,0:T(4,128)S(1)} %pad_maximum_fusion.9), channel_id=1, source_target_pairs={{0,2},{1,3},{2,0},{3,1},{4,6},{5,7},{6,4},{7,5},{8,10},{9,11},{10,... | collective-permute-start | bytes 25928 | tf_op jit(solution)/shard_map/ppermute | solution.py:163
  128.4 5.2 %collective-permute-start.5 = (f32[2,2,3,180]{3,2,1,0:T(4,128)S(1)}, f32[2,2,3,180]{3,2,1,0:T(4,128)S(1)}, u32[]{:S(2)}, u32[]{:S(2)}) collective-permute-start(f32[2,2,3,180]{3,2,1,0:T(4,128)S(1)} %pad_maximum_fusion.9), channel_id=1, source_target_pairs={{0,1},{1,2},{2,3},{3,0},{4,5},{5,6},{6,7},{7,4},{8,9},{9,10},{10,1... | collective-permute-start | bytes 25928 | tf_op jit(solution)/shard_map/ppermute | solution.py:163
  128.6 5.0 %collective-permute-start.3 = (f32[2,2,3,180]{3,2,1,0:T(4,128)S(1)}, f32[2,2,3,180]{3,2,1,0:T(4,128)S(1)}, u32[]{:S(2)}, u32[]{:S(2)}) collective-permute-start(f32[2,2,3,180]{3,2,1,0:T(4,128)S(1)} %pad_maximum_fusion.9), channel_id=1, source_target_pairs={{0,3},{1,0},{2,1},{3,2},{4,7},{5,4},{6,5},{7,6},{8,11},{9,8},{10,9... | collective-permute-start | bytes 25928 | tf_op jit(solution)/shard_map/ppermute | solution.py:163
  176.9 2.1 copy-start.5
  179.3 1.0 copy-start.10
  180.7 17.0 %copy-start.13 = (bf16[2,3,180,256]{3,2,1,0:T(8,128)(2,1)S(1)}, bf16[2,3,180,256]{3,2,1,0:T(8,128)(2,1)}, u32[]{:S(2)}) copy-start(bf16[2,3,180,256]{3,2,1,0:T(8,128)(2,1)} %reduce-scatter.5.cloned.1.call-done) | copy-start | bytes 1658884
  181.3 16.4 %copy-start.4 = (bf16[2,3,180,256]{3,0,2,1:T(2,128)(2,1)S(1)}, bf16[2,3,180,256]{3,0,2,1:T(2,128)(2,1)}, u32[]{:S(2)}) copy-start(bf16[2,3,180,256]{3,0,2,1:T(2,128)(2,1)} %param.8) | copy-start | bytes 1658884
  181.3 16.4 %copy-start.7 = (bf16[2,3,180,256]{3,2,1,0:T(8,128)(2,1)S(1)}, bf16[2,3,180,256]{3,2,1,0:T(8,128)(2,1)}, u32[]{:S(2)}) copy-start(bf16[2,3,180,256]{3,2,1,0:T(8,128)(2,1)} %fusion.37) | copy-start | bytes 1658884
  181.3 16.4 %copy-start.9 = (bf16[2,3,180,256]{3,0,2,1:T(2,128)(2,1)S(1)}, bf16[2,3,180,256]{3,0,2,1:T(2,128)(2,1)}, u32[]{:S(2)}) copy-start(bf16[2,3,180,256]{3,0,2,1:T(2,128)(2,1)} %param.9) | copy-start | bytes 1658884
  181.3 16.4 %copy-start.12 = (f32[2,180,96]{2,1,0:T(8,128)S(1)}, f32[2,180,96]{2,1,0:T(8,128)}, u32[]{:S(2)}) copy-start(f32[2,180,96]{2,1,0:T(8,128)} %copy-done.11) | copy-start | bytes 414724
  200.5 5.3 %collective-permute-start.7 = (f32[2,2,3,180]{3,2,1,0:T(4,128)S(1)}, f32[2,2,3,180]{3,2,1,0:T(4,128)S(1)}, u32[]{:S(2)}, u32[]{:S(2)}) collective-permute-start(f32[2,2,3,180]{3,2,1,0:T(4,128)S(1)} %pad_maximum_fusion.10), channel_id=1, source_target_pairs={{0,2},{1,3},{2,0},{3,1},{4,6},{5,7},{6,4},{7,5},{8,10},{9,11},{10,... | collective-permute-start | bytes 25928 | tf_op jit(solution)/shard_map/ppermute | solution.py:163
  202.0 4.9 %collective-permute-start.8 = (f32[2,2,3,180]{3,2,1,0:T(4,128)S(1)}, f32[2,2,3,180]{3,2,1,0:T(4,128)S(1)}, u32[]{:S(2)}, u32[]{:S(2)}) collective-permute-start(f32[2,2,3,180]{3,2,1,0:T(4,128)S(1)} %pad_maximum_fusion.10), channel_id=1, source_target_pairs={{0,1},{1,2},{2,3},{3,0},{4,5},{5,6},{6,7},{7,4},{8,9},{9,10},{10,1... | collective-permute-start | bytes 25928 | tf_op jit(solution)/shard_map/ppermute | solution.py:163
  202.4 4.6 %collective-permute-start.6 = (f32[2,2,3,180]{3,2,1,0:T(4,128)S(1)}, f32[2,2,3,180]{3,2,1,0:T(4,128)S(1)}, u32[]{:S(2)}, u32[]{:S(2)}) collective-permute-start(f32[2,2,3,180]{3,2,1,0:T(4,128)S(1)} %pad_maximum_fusion.10), channel_id=1, source_target_pairs={{0,3},{1,0},{2,1},{3,2},{4,7},{5,4},{6,5},{7,6},{8,11},{9,8},{10,9... | collective-permute-start | bytes 25928 | tf_op jit(solution)/shard_map/ppermute | solution.py:163
Sparse Core Ops, SparseCore 0:
  15.7 35.1 all-gather.2
  76.0 31.6 all-gather.4
  118.7 32.1 reduce-scatter.4
  153.4 30.7 reduce-scatter.2
